TPU v7x, 32 devices: a whole 2x2x4 slice. The times are simulated.
32 devices in a mesh: rep: 8 (over z, core), tp: 4 (over y, x).
Axes of the slice: x: 2, y: 2, z: 4, core: 2. Of those that a mesh axis runs over, the one named last changes fastest.
Arguments:
- partials: bfloat16 [512, 32768], P('rep', 'tp'), may hold values from -6 to 6
- residual: bfloat16 [512, 8192], P('rep', 'tp'), may hold values from -6 to 6
- lower: bfloat16 [512, 8192], P('rep', 'tp'), may hold values from -6 to 6
- middle: bfloat16 [512, 8192], P('rep', 'tp'), may hold values from -6 to 6
- accepted: int32 [256], P('rep'), may hold values from 0 to 63
- fc_weight: bfloat16 [3, 8192, 8192], P(None, 'rep', 'tp')
- norm_gain: float32 [8192], P('tp'), may hold values from 0.1 to 1.9
- grad_normed: bfloat16 [256, 8192], P('rep', 'tp')
Outputs:
- normed: bfloat16 [256, 8192], P('rep', 'tp')
- grad_fc: bfloat16 [3, 8192, 8192], P(None, 'rep', 'tp')
All inputs are finite; a program needn't handle non-finite values.
Results may differ from a plain program's by a relative error of at most 0.017.
Values may be sent and summed in bfloat16 or wider, within the bound.
No kernel may reach another device: no remote copies, remote signals or barrier semaphores. Data moves between devices by JAX's collectives and lax.ppermute only.
A program may use at most 64 MiB of HBM per device.

v0:
```python
import jax
import jax.numpy as jnp
from jax import lax
from jax.sharding import PartitionSpec as P

D = 8192


EPSILON = 1e-06


def from_root(shard, axis, root):
    mine = lax.axis_index(axis) == root
    return lax.psum(jnp.where(mine, shard, jnp.zeros_like(shard)), axis)


def body(partials, residual, lower, middle, accepted, fc_weight, norm_gain, grad_normed):
    picked = jnp.take(partials, accepted, axis=0).astype(jnp.float32)
    summed = lax.psum_scatter(
        picked.astype(jnp.bfloat16), "tp", scatter_dimension=1, tiled=True
    ).astype(jnp.float32)
    upper_rows = (jnp.take(residual, accepted, axis=0).astype(jnp.float32) + summed).astype(
        jnp.bfloat16
    )
    local_rows = jnp.stack(
        [jnp.take(lower, accepted, axis=0), jnp.take(middle, accepted, axis=0), upper_rows], axis=1
    )
    rep_count = lax.axis_size("rep")
    tp_count = lax.axis_size("tp")
    group_ratio = rep_count // tp_count
    slab_width = D // rep_count
    gathered = lax.all_gather(local_rows, "rep", axis=0, tiled=True)
    rep_index = lax.axis_index("rep")
    portion = lax.dynamic_slice_in_dim(
        gathered, rep_index % group_ratio * slab_width, slab_width, 2
    )
    features = from_root(portion, "tp", rep_index // group_ratio)
    total_rows = features.shape[0]
    feature_flat = features.reshape(total_rows, 3 * slab_width)
    fc_block = fc_weight.reshape(3 * slab_width, fc_weight.shape[2])
    hidden = lax.psum_scatter(
        jnp.dot(feature_flat, fc_block, preferred_element_type=jnp.float32),
        "rep",
        scatter_dimension=0,
        tiled=True,
    )
    squares = lax.psum(jnp.sum(hidden * hidden, axis=1), "tp")
    inv_rms = lax.rsqrt(squares / D + EPSILON)
    normed = (hidden * inv_rms[:, None] * norm_gain).astype(jnp.bfloat16)
    scaled = grad_normed.astype(jnp.float32) * norm_gain
    inner_sum = lax.psum(jnp.sum(scaled * hidden, axis=1), "tp")
    hidden_grads = (
        inv_rms[:, None] * scaled - hidden * (inv_rms**3 * inner_sum / D)[:, None]
    ).astype(jnp.bfloat16)
    hidden_grads_all = lax.all_gather(hidden_grads, "rep", axis=0, tiled=True)
    grad_fc = lax.dot_general(
        feature_flat, hidden_grads_all, (((0,), (0,)), ((), ())), preferred_element_type=jnp.float32
    )
    grad_fc = grad_fc.reshape(fc_weight.shape).astype(jnp.bfloat16)
    return (normed, grad_fc)


def solution(mesh):
    in_specs = (
        P("rep", "tp"),
        P("rep", "tp"),
        P("rep", "tp"),
        P("rep", "tp"),
        P("rep"),
        P(None, "rep", "tp"),
        P("tp"),
        P("rep", "tp"),
    )
    out_specs = (P("rep", "tp"), P(None, "rep", "tp"))
    return jax.shard_map(body, mesh=mesh, in_specs=in_specs, out_specs=out_specs, check_vma=False)
```

profile of v0, /device:TPU:0, one launch (start us, length us, event | category | flops | bytes accessed | tf_op | source)
XLA Modules:
  0.0 234.9 jit_solution(5484597971541123946)
XLA Ops:
  7.2 0.0 copy-start
  7.2 0.0 reduce-scatter.3.cloned.1.call-start
  7.2 0.7 compare_and_fusion
  8.0 0.7 compare_select_fusion
  8.6 0.0 copy-done
  8.6 0.9 gather_fusion
  9.5 0.0 copy-start.1
  9.5 0.0 copy-start.2
  9.5 0.9 broadcast_select_fusion
  10.5 0.0 copy-start.3
  10.5 0.0 reduce-scatter.3.cloned.1.call-update
  10.5 0.0 all-gather.3.cloned.1.call-start
  10.5 0.0 copy-done.1
  10.5 0.7 gather_fusion.3
  11.2 0.0 copy-done.2
  11.2 0.7 gather_fusion.2
  11.9 0.0 copy-done.3
  11.9 0.7 gather_fusion.1
  12.5 0.1 select_bitcast_fusion.1
  12.6 26.6 %reduce-scatter.3.cloned.1.call-done = bf16[32,2048]{1,0:T(8,128)(2,1)} async-done(((bf16[32,8192]{1,0:T(8,128)(2,1)}), bf16[32,2048]{1,0:T(8,128)(2,1)}) %reduce-scatter.3.cloned.1.call-update) | async-done | bytes 131088 | tf_op jit(solution)/shard_map/reduce_scatter | solution.py:19
  39.2 1.0 fusion.2
  40.2 0.8 pad_maximum_fusion
  41.0 0.0 all-gather.3.cloned.1.call-update
  41.1 0.0 all-reduce.3.cloned.1.call-start
  41.1 38.5 %all-gather.3.cloned.1.call-done = bf16[256,3,2048]{2,0,1:T(8,128)(2,1)} async-done(((bf16[32,3,2048]{2,0,1:T(8,128)(2,1)}), bf16[256,3,2048]{2,0,1:T(8,128)(2,1)}) %all-gather.3.cloned.1.call-update) | async-done | bytes 3145744 | tf_op jit(solution)/shard_map/all_gather | solution.py:32
  79.7 2.9 %dynamic-slice_select_fusion = bf16[256,3,1024]{2,0,1:T(8,128)(2,1)} fusion(bf16[256,3,2048]{2,0,1:T(8,128)(2,1)} %all-gather.3.cloned.1.call-done, s32[]{:T(128)S(6)} %select_n.42, pred[]{:T(512)S(6)} %eq.5), kind=kLoop, calls=%fused_computation.7 | loop fusion | flops 786432 | bytes 3145733 | tf_op jit(solution)/shard_map/jit(_where)/select_n | solution.py:14
  82.6 0.0 all-reduce.3.cloned.1.call-update
  82.6 0.0 reduce-scatter.5.cloned.1.call-start
  82.7 60.3 %all-reduce.3.cloned.1.call-done = bf16[256,3,1024]{2,0,1:T(8,128)(2,1)} async-done(((bf16[256,3,1024]{2,0,1:T(8,128)(2,1)}), bf16[256,3,1024]{2,0,1:T(8,128)(2,1)}) %all-reduce.3.cloned.1.call-update) | async-done | bytes 1572880 | tf_op jit(solution)/shard_map/psum | solution.py:14
  143.0 9.8 %convolution_bitcast_fusion = f32[256,2048]{1,0:T(8,128)} fusion(bf16[256,3,1024]{2,0,1:T(8,128)(2,1)} %all-reduce.3.cloned.1.call-done, bf16[3,1024,2048]{2,1,0:T(8,128)(2,1)} %param.15), kind=kOutput, calls=%fused_computation.5 | convolution fusion | flops 3221225472 | bytes 16252928 | tf_op jit(solution)/shard_map/dot_general | solution.py:42
  152.8 0.0 copy-start.4
  152.8 0.0 copy-start.5
  152.8 0.0 reduce-scatter.5.cloned.1.call-update
  152.8 0.0 all-gather.5.cloned.1.call-start
  152.9 36.1 %reduce-scatter.5.cloned.1.call-done = f32[32,2048]{1,0:T(8,128)} async-done(((f32[256,2048]{1,0:T(8,128)}), f32[32,2048]{1,0:T(8,128)}) %reduce-scatter.5.cloned.1.call-update) | async-done | bytes 262160 | tf_op jit(solution)/shard_map/reduce_scatter | solution.py:41
  189.0 0.0 copy-done.4
  189.0 0.0 copy-done.5
  189.0 1.1 multiply_reduce_fusion
  190.1 9.8 %all-reduce = (f32[32]{0:T(128)S(1)}, f32[32]{0:T(128)S(1)}) all-reduce(f32[32]{0:T(128)S(1)} %get-tuple-element.4, f32[32]{0:T(128)S(1)} %get-tuple-element.3), channel_id=1, replica_groups=mesh['rep'=8,'tp'=4] {'tp'}, use_global_device_ids=true, to_apply=%region_4.6 | all-reduce | flops 64 | bytes 512 | tf_op jit(solution)/shard_map/psum | solution.py:47
  200.0 1.8 subtract_convert_fusion
  201.8 0.0 all-gather.5.cloned.1.call-update
  201.8 1.7 copy.10
  203.5 17.0 %all-gather.5.cloned.1.call-done = bf16[256,2048]{1,0:T(8,128)(2,1)} async-done(((bf16[32,2048]{1,0:T(8,128)(2,1)}), bf16[256,2048]{1,0:T(8,128)(2,1)}) %all-gather.5.cloned.1.call-update) | async-done | bytes 1048592 | tf_op jit(solution)/shard_map/all_gather | solution.py:55
  220.5 7.8 %convolution_convert_fusion = bf16[3,1024,2048]{2,1,0:T(8,128)(2,1)} fusion(bf16[256,3,1024]{0,2,1:T(8,128)(2,1)S(1)} %copy.10, bf16[256,2048]{1,0:T(8,128)(2,1)} %all-gather.5.cloned.1.call-done), kind=kOutput, calls=%fused_computation.4 | convolution fusion | flops 3227516928 | bytes 15204352 | tf_op jit(solution)/shard_map/dot_general | solution.py:56
  (2 shorter events, 0.0 us)
Async XLA Ops:
  7.2 1.5 copy-start
  7.2 32.0 %reduce-scatter.3.cloned.1.call-start = ((), (), s32[]{:S(2)}) async-start(), calls=%async_computation.2 | async-start | bytes 655360 | tf_op jit(solution)/shard_map/reduce_scatter | solution.py:19
  9.5 1.0 copy-start.1
  9.5 1.7 copy-start.2
  10.5 1.4 copy-start.3
  10.5 69.2 %all-gather.3.cloned.1.call-start = ((), (), s32[]{:S(2)}) async-start(), calls=%async_computation.3 | async-start | bytes 3538944 | tf_op jit(solution)/shard_map/all_gather | solution.py:32
  41.1 102.0 %all-reduce.3.cloned.1.call-start = ((), (), s32[]{:S(2)}) async-start(), calls=%async_computation.4 | async-start | bytes 3145728 | tf_op jit(solution)/shard_map/psum | solution.py:14
  82.6 106.4 %reduce-scatter.5.cloned.1.call-start = ((), (), s32[]{:S(2)}) async-start(), calls=%async_computation.5 | async-start | bytes 2359296 | tf_op jit(solution)/shard_map/reduce_scatter | solution.py:41
  152.8 36.2 %copy-start.4 = (bf16[32,2048]{1,0:T(8,128)(2,1)S(1)}, bf16[32,2048]{1,0:T(8,128)(2,1)}, u32[]{:S(2)}) copy-start(bf16[32,2048]{1,0:T(8,128)(2,1)} %param.17) | copy-start | bytes 393220
  152.8 36.2 %copy-start.5 = (f32[2048]{0:T(1024)S(1)}, f32[2048]{0:T(1024)}, u32[]{:S(2)}) copy-start(f32[2048]{0:T(1024)} %param.16) | copy-start | bytes 24580
  152.8 67.7 %all-gather.5.cloned.1.call-start = ((), (), s32[]{:S(2)}) async-start(), calls=%async_computation.6 | async-start | bytes 1179648 | tf_op jit(solution)/shard_map/all_gather | solution.py:55
Sparse Core Ops, SparseCore 0:
  11.4 27.8 reduce-scatter.2
  41.4 38.2 all-gather.2
  83.3 59.6 all-reduce.2
  153.0 36.0 reduce-scatter.4
  201.9 18.5 all-gather.4
where the time goes:
time: 235 us
  waiting for transfers between devices  179 us (76%)
  matrix products  17.6 us (7%)
  between operations  13.9 us (6%)
  other arithmetic  10.1 us (4%)
  blocking collectives  9.84 us (4%)
  local copies, waits for them, and re-layouts  4.57 us (2%)
    psum x1, waiting for transfers between devices, from_root(): return lax.psum(jnp.where(mine, shard, jnp.zeros_like(shard)), axis)  60.3 us
    all_gather x1, waiting for transfers between devices, body(): gathered = lax.all_gather(local_rows, 'rep', axis=0, tiled=True)  38.5 us
    reduce_scatter x1, waiting for transfers between devices, body(): lax.psum_scatter(jnp.dot(feature_flat, fc_block, preferred_element_type=j...  36.1 us
    reduce_scatter x1, waiting for transfers between devices, body(): lax.psum_scatter(picked.astype(jnp.bfloat16), 'tp', scatter_dimension=1,...  26.6 us
    all_gather x1, waiting for transfers between devices, body(): hidden_grads_all = lax.all_gather(hidden_grads, 'rep', axis=0, tiled=True)  17 us
    psum x1, blocking collectives, body(): squares = lax.psum(jnp.sum(hidden * hidden, axis=1), 'tp')  9.84 us
    dot_general x1, matrix products, body(): jnp.dot(feature_flat, fc_block, preferred_element_type=jnp.float32)  9.79 us
    dot_general x1, matrix products, body(): lax.dot_general(feature_flat, hidden_grads_all, (((0,), (0,)), ((), ())),...  7.81 us
  transfers between devices with their start and end apart: 5, of which 5 were waited for; matrix products, arithmetic and copies ran while one was open for 2% of the time, Pallas kernels for 0%

commit v1 on v0

--- a/solution.py
+++ b/solution.py
@@ -9,32 +9,48 @@
 EPSILON = 1e-06
 
 
-def from_root(shard, axis, root):
-    mine = lax.axis_index(axis) == root
-    return lax.psum(jnp.where(mine, shard, jnp.zeros_like(shard)), axis)
+def xor_exchange(chunk_of, axis, size):
+    for k in range(1, size):
+        perm = [(i, i ^ k) for i in range(size)]
+        yield lax.ppermute(chunk_of(k), axis, perm)
 
 
 def body(partials, residual, lower, middle, accepted, fc_weight, norm_gain, grad_normed):
-    picked = jnp.take(partials, accepted, axis=0).astype(jnp.float32)
-    summed = lax.psum_scatter(
-        picked.astype(jnp.bfloat16), "tp", scatter_dimension=1, tiled=True
-    ).astype(jnp.float32)
+    rep_count = lax.axis_size("rep")
+    tp_count = lax.axis_size("tp")
+    rep_index = lax.axis_index("rep")
+    tp_index = lax.axis_index("tp")
+    rows = accepted.shape[0]
+    tp_width = residual.shape[1]
+
+    picked = jnp.take(partials, accepted, axis=0).reshape(rows, tp_count, tp_width)
+    summed = jnp.take(picked, tp_index, axis=1).astype(jnp.float32)
+    for got in xor_exchange(lambda k: jnp.take(picked, tp_index ^ k, axis=1), "tp", tp_count):
+        summed = summed + got.astype(jnp.float32)
     upper_rows = (jnp.take(residual, accepted, axis=0).astype(jnp.float32) + summed).astype(
         jnp.bfloat16
     )
     local_rows = jnp.stack(
         [jnp.take(lower, accepted, axis=0), jnp.take(middle, accepted, axis=0), upper_rows], axis=1
     )
-    rep_count = lax.axis_size("rep")
-    tp_count = lax.axis_size("tp")
-    group_ratio = rep_count // tp_count
+
     slab_width = D // rep_count
-    gathered = lax.all_gather(local_rows, "rep", axis=0, tiled=True)
-    rep_index = lax.axis_index("rep")
-    portion = lax.dynamic_slice_in_dim(
-        gathered, rep_index % group_ratio * slab_width, slab_width, 2
-    )
-    features = from_root(portion, "tp", rep_index // group_ratio)
+    group = rep_count // tp_count
+    slabs = local_rows.reshape(rows, 3, group, slab_width)
+    received = []
+    for c in range(group):
+        perm = []
+        for r in range(rep_count):
+            for t in range(tp_count):
+                s = group * t + (r - c) % group
+                perm.append((r * tp_count + t, s * tp_count + r // group))
+        block = jnp.take(slabs, (rep_index - c) % group, axis=2)
+        received.append(lax.ppermute(block, ("rep", "tp"), perm))
+    stacked = jnp.stack(received, axis=0)
+    order = (jnp.arange(group, dtype=jnp.int32) - rep_index) % group
+    mine = jnp.take(stacked, order, axis=0).reshape(group * rows, 3, slab_width)
+    features = lax.all_gather(mine, "tp", axis=0, tiled=True)
+
     total_rows = features.shape[0]
     feature_flat = features.reshape(total_rows, 3 * slab_width)
     fc_block = fc_weight.reshape(3 * slab_width, fc_weight.shape[2])

time: 235 us -> 175 us (0.74)
  waiting for transfers between devices: 179 us -> 117 us
  starting transfers between devices: 0.21 us -> 5.44 us
  other arithmetic: 10.1 us -> 5.65 us
    psum x1 -> x0, waiting for transfers between devices: 60.3 us -> none  [from_root(): return lax.psum(jnp.where(mine, shard, jnp.zeros_like(shard)), axis)]
    reduce_scatter x1 -> x0, waiting for transfers between devices: 26.6 us -> none  [body(): lax.psum_scatter(picked.astype(jnp.bfloat16), 'tp', scatter_dimension=1,...]
    all_gather x1, waiting for transfers between devices: 38.5 us -> 57.1 us  [body(): features = lax.all_gather(mine, 'tp', axis=0, tiled=True)]
    ppermute x0 -> x5, waiting for transfers between devices: none -> 6.31 us  [the longest x3 4.92 us: xor_exchange(): yield lax.ppermute(chunk_of(k), axis, perm)]
    ppermute x0 -> x5, starting transfers between devices: none -> 5.32 us  [the longest x3 4.57 us: xor_exchange(): yield lax.ppermute(chunk_of(k), axis, perm)]
    select_n x2 -> x6, other arithmetic: 3.85 us -> 1.17 us  [the longest x2 0.86 us: body(): mine = jnp.take(stacked, order, axis=0).reshape(group * rows, 3, slab_width)]
  transfers between devices with their start and end apart: 5 -> 8, of which waited for: 5 -> 6; matrix products, arithmetic and copies ran while one was open for 2% -> 2% of each run, Pallas kernels for 0% -> 0%
where the time goes in v1:
time: 175 us
  waiting for transfers between devices  117 us (67%)
  matrix products  17.6 us (10%)
  between operations  14 us (8%)
  blocking collectives  9.79 us (6%)
  local copies, waits for them, and re-layouts  5.65 us (3%)
  other arithmetic  5.65 us (3%)
  starting transfers between devices  5.44 us (3%)
    all_gather x1, waiting for transfers between devices, body(): features = lax.all_gather(mine, 'tp', axis=0, tiled=True)  57.1 us
    reduce_scatter x1, waiting for transfers between devices, body(): lax.psum_scatter(jnp.dot(feature_flat, fc_block, preferred_element_type=j...  36.2 us
    all_gather x1, waiting for transfers between devices, body(): hidden_grads_all = lax.all_gather(hidden_grads, 'rep', axis=0, tiled=True)  17 us
    psum x1, blocking collectives, body(): squares = lax.psum(jnp.sum(hidden * hidden, axis=1), 'tp')  9.79 us
    dot_general x1, matrix products, body(): jnp.dot(feature_flat, fc_block, preferred_element_type=jnp.float32)  9.79 us
    dot_general x1, matrix products, body(): lax.dot_general(feature_flat, hidden_grads_all, (((0,), (0,)), ((), ())),...  7.8 us
    ppermute x3, waiting for transfers between devices, xor_exchange(): yield lax.ppermute(chunk_of(k), axis, perm)  4.92 us
    ppermute x3, starting transfers between devices, xor_exchange(): yield lax.ppermute(chunk_of(k), axis, perm)  4.57 us
  transfers between devices with their start and end apart: 8, of which 6 were waited for; matrix products, arithmetic and copies ran while one was open for 2% of the time, Pallas kernels for 0%

profile of v1, /device:TPU:0, one launch (start us, length us, event | category | flops | bytes accessed | tf_op | source)
XLA Modules:
  0.0 174.8 jit_solution(10353855674359227189)
XLA Ops:
  7.2 0.0 copy-start
  7.2 0.0 all-gather.3.cloned.1.call-start
  7.3 0.7 compare_and_fusion
  8.0 0.7 compare_select_fusion
  8.7 0.0 copy-done
  8.7 0.9 gather_fusion
  9.5 0.0 copy-start.1
  9.6 0.0 copy-start.2
  9.6 0.0 copy-start.3
  9.6 0.1 bitcast_select_fusion
  9.8 3.0 %collective-permute-start = (bf16[32,2048]{1,0:T(8,128)(2,1)S(1)}, bf16[32,2048]{1,0:T(8,128)(2,1)S(1)}, u32[]{:S(2)}, u32[]{:S(2)}) collective-permute-start(bf16[32,2048]{1,0:T(8,128)(2,1)S(1)} %get-tuple-element.31), channel_id=1, source_target_pairs={{0,1},{1,0},{2,3},{3,2},{4,5},{5,4},{6,7},{7,6},{8,9},{9,8},{10,11... | collective-permute-start | bytes 393224 | tf_op jit(solution)/shard_map/ppermute | solution.py:15
  12.8 1.5 collective-permute-start.2
  14.3 0.1 collective-permute-start.1
  14.3 0.1 broadcast_in_dim.58
  14.4 0.1 broadcast_in_dim.59
  14.5 0.0 copy-done.1
  14.5 0.6 gather_fusion.4
  15.2 0.0 copy-done.2
  15.2 0.7 gather_fusion.3
  15.8 0.0 copy-done.3
  15.8 0.7 gather_fusion.2
  16.5 0.1 broadcast_select_fusion
  16.6 0.1 stack.22
  16.7 0.1 stack.21
  16.8 0.0 collective-permute-done
  16.9 3.6 %collective-permute-done.2 = bf16[32,2048]{1,0:T(8,128)(2,1)S(1)} collective-permute-done((bf16[32,2048]{1,0:T(8,128)(2,1)S(1)}, bf16[32,2048]{1,0:T(8,128)(2,1)S(1)}, u32[]{:S(2)}, u32[]{:S(2)}) %collective-permute-start.2) | collective-permute-done | bytes 131104 | tf_op jit(solution)/shard_map/ppermute | solution.py:15
  20.4 1.4 collective-permute-done.1
  21.8 0.1 add_convert_fusion
  21.9 0.1 stack.23
  22.1 0.7 collective-permute-start.3
  22.7 0.1 collective-permute-start.4
  22.8 0.0 collective-permute-done.3
  22.9 1.4 collective-permute-done.4
  24.3 0.6 gather_fusion.1
  24.9 0.9 bitcast_select_fusion.1
  25.8 0.0 all-gather.3.cloned.1.call-update
  25.8 0.0 reduce-scatter.2.cloned.1.call-start
  25.8 57.1 %all-gather.3.cloned.1.call-done = bf16[256,3,1024]{2,0,1:T(8,128)(2,1)} async-done(((bf16[64,3,1024]{2,0,1:T(8,128)(2,1)}), bf16[256,3,1024]{2,0,1:T(8,128)(2,1)}) %all-gather.3.cloned.1.call-update) | async-done | bytes 1572880 | tf_op jit(solution)/shard_map/all_gather | solution.py:52
  82.9 9.8 %convolution_bitcast_fusion = f32[256,2048]{1,0:T(8,128)} fusion(bf16[256,3,1024]{2,0,1:T(8,128)(2,1)} %all-gather.3.cloned.1.call-done, bf16[3,1024,2048]{2,1,0:T(8,128)(2,1)} %param.19), kind=kOutput, calls=%fused_computation.6 | convolution fusion | flops 3221225472 | bytes 16252928 | tf_op jit(solution)/shard_map/dot_general | solution.py:58
  92.7 0.0 copy-start.4
  92.7 0.0 copy-start.5
  92.7 0.0 reduce-scatter.2.cloned.1.call-update
  92.8 0.0 all-gather.5.cloned.1.call-start
  92.8 36.2 %reduce-scatter.2.cloned.1.call-done = f32[32,2048]{1,0:T(8,128)} async-done(((f32[256,2048]{1,0:T(8,128)}), f32[32,2048]{1,0:T(8,128)}) %reduce-scatter.2.cloned.1.call-update) | async-done | bytes 262160 | tf_op jit(solution)/shard_map/reduce_scatter | solution.py:57
  129.0 0.0 copy-done.4
  129.0 0.0 copy-done.5
  129.0 1.1 multiply_reduce_fusion
  130.1 9.8 %all-reduce = (f32[32]{0:T(128)S(1)}, f32[32]{0:T(128)S(1)}) all-reduce(f32[32]{0:T(128)S(1)} %get-tuple-element.28, f32[32]{0:T(128)S(1)} %get-tuple-element.27), channel_id=1, replica_groups=mesh['rep'=8,'tp'=4] {'tp'}, use_global_device_ids=true, to_apply=%region_2.6 | all-reduce | flops 64 | bytes 512 | tf_op jit(solution)/shard_map/psum | solution.py:63
  139.9 1.8 %subtract_convert_fusion = (bf16[32,2048]{1,0:T(8,128)(2,1)}, bf16[32,2048]{1,0:T(8,128)(2,1)}) fusion(f32[32,2048]{1,0:T(8,128)} %reduce-scatter.2.cloned.1.call-done, bf16[32,2048]{1,0:T(8,128)(2,1)S(1)} %copy-done.4, f32[32]{0:T(128)S(1)} %get-tuple-element.38, f32[2048]{0:T(1024)S(1)} %copy-done.5, f32[32]{0:T(128)S(1)} %get-tuple-element.39), kind=kLoop, calls=%fused_computation.12 | loop fusion | flops 589824 | bytes 663808 | tf_op jit(solution)/shard_map/convert_element_type | solution.py:70
  141.7 0.0 all-gather.5.cloned.1.call-update
  141.7 1.7 copy.16
  143.4 17.0 %all-gather.5.cloned.1.call-done = bf16[256,2048]{1,0:T(8,128)(2,1)} async-done(((bf16[32,2048]{1,0:T(8,128)(2,1)}), bf16[256,2048]{1,0:T(8,128)(2,1)}) %all-gather.5.cloned.1.call-update) | async-done | bytes 1048592 | tf_op jit(solution)/shard_map/all_gather | solution.py:71
  160.5 7.8 %convolution_convert_fusion = bf16[3,1024,2048]{2,1,0:T(8,128)(2,1)} fusion(bf16[256,3,1024]{0,2,1:T(8,128)(2,1)S(1)} %copy.16, bf16[256,2048]{1,0:T(8,128)(2,1)} %all-gather.5.cloned.1.call-done), kind=kOutput, calls=%fused_computation.5 | convolution fusion | flops 3227516928 | bytes 15204352 | tf_op jit(solution)/shard_map/dot_general | solution.py:72
  (12 shorter events, 0.3 us)
Async XLA Ops:
  7.2 1.5 copy-start
  7.2 75.8 %all-gather.3.cloned.1.call-start = ((), (), s32[]{:S(2)}) async-start(), calls=%async_computation.1 | async-start | bytes 1966080 | tf_op jit(solution)/shard_map/all_gather | solution.py:52
  9.5 5.0 %copy-start.1 = (bf16[64,2048]{1,0:T(8,128)(2,1)S(1)}, bf16[64,2048]{1,0:T(8,128)(2,1)}, u32[]{:S(2)}) copy-start(bf16[64,2048]{1,0:T(8,128)(2,1)} %param.15) | copy-start | bytes 786436
  9.6 5.6 %copy-start.2 = (bf16[64,2048]{1,0:T(8,128)(2,1)S(1)}, bf16[64,2048]{1,0:T(8,128)(2,1)}, u32[]{:S(2)}) copy-start(bf16[64,2048]{1,0:T(8,128)(2,1)} %param.17) | copy-start | bytes 786436
  9.6 6.3 %copy-start.3 = (bf16[64,2048]{1,0:T(8,128)(2,1)S(1)}, bf16[64,2048]{1,0:T(8,128)(2,1)}, u32[]{:S(2)}) copy-start(bf16[64,2048]{1,0:T(8,128)(2,1)} %param.16) | copy-start | bytes 786436
  9.8 7.1 %collective-permute-start = (bf16[32,2048]{1,0:T(8,128)(2,1)S(1)}, bf16[32,2048]{1,0:T(8,128)(2,1)S(1)}, u32[]{:S(2)}, u32[]{:S(2)}) collective-permute-start(bf16[32,2048]{1,0:T(8,128)(2,1)S(1)} %get-tuple-element.31), channel_id=1, source_target_pairs={{0,1},{1,0},{2,3},{3,2},{4,5},{5,4},{6,7},{7,6},{8,9},{9,8},{10,11... | collective-permute-start | bytes 393224 | tf_op jit(solution)/shard_map/ppermute | solution.py:15
  12.8 7.6 %collective-permute-start.2 = (bf16[32,2048]{1,0:T(8,128)(2,1)S(1)}, bf16[32,2048]{1,0:T(8,128)(2,1)S(1)}, u32[]{:S(2)}, u32[]{:S(2)}) collective-permute-start(bf16[32,2048]{1,0:T(8,128)(2,1)S(1)} %get-tuple-element.32), channel_id=1, source_target_pairs={{0,3},{1,2},{2,1},{3,0},{4,7},{5,6},{6,5},{7,4},{8,11},{9,10},{10,... | collective-permute-start | bytes 393224 | tf_op jit(solution)/shard_map/ppermute | solution.py:15
  14.3 7.5 %collective-permute-start.1 = (bf16[32,2048]{1,0:T(8,128)(2,1)S(1)}, bf16[32,2048]{1,0:T(8,128)(2,1)S(1)}, u32[]{:S(2)}, u32[]{:S(2)}) collective-permute-start(bf16[32,2048]{1,0:T(8,128)(2,1)S(1)} %get-tuple-element.33), channel_id=1, source_target_pairs={{0,2},{1,3},{2,0},{3,1},{4,6},{5,7},{6,4},{7,5},{8,10},{9,11},{10,... | collective-permute-start | bytes 393224 | tf_op jit(solution)/shard_map/ppermute | solution.py:15
  22.1 0.8 collective-permute-start.3
  22.7 1.5 collective-permute-start.4
  25.8 103.2 %reduce-scatter.2.cloned.1.call-start = ((), (), s32[]{:S(2)}) async-start(), calls=%async_computation.2 | async-start | bytes 2359296 | tf_op jit(solution)/shard_map/reduce_scatter | solution.py:57
  92.7 36.3 %copy-start.4 = (bf16[32,2048]{1,0:T(8,128)(2,1)S(1)}, bf16[32,2048]{1,0:T(8,128)(2,1)}, u32[]{:S(2)}) copy-start(bf16[32,2048]{1,0:T(8,128)(2,1)} %param.21) | copy-start | bytes 393220
  92.7 36.3 %copy-start.5 = (f32[2048]{0:T(1024)S(1)}, f32[2048]{0:T(1024)}, u32[]{:S(2)}) copy-start(f32[2048]{0:T(1024)} %param.20) | copy-start | bytes 24580
  92.8 67.7 %all-gather.5.cloned.1.call-start = ((), (), s32[]{:S(2)}) async-start(), calls=%async_computation.3 | async-start | bytes 1179648 | tf_op jit(solution)/shard_map/all_gather | solution.py:71
Sparse Core Ops, SparseCore 0:
  25.9 56.9 all-gather.2
  92.9 36.0 reduce-scatter.1
  141.8 18.5 all-gather.4

commit v2 on v1

--- a/solution.py
+++ b/solution.py
@@ -49,7 +49,10 @@
     stacked = jnp.stack(received, axis=0)
     order = (jnp.arange(group, dtype=jnp.int32) - rep_index) % group
     mine = jnp.take(stacked, order, axis=0).reshape(group * rows, 3, slab_width)
-    features = lax.all_gather(mine, "tp", axis=0, tiled=True)
+    pieces = [mine] + list(xor_exchange(lambda k: mine, "tp", tp_count))
+    source = tp_index ^ jnp.arange(tp_count, dtype=jnp.int32)
+    features = jnp.take(jnp.stack(pieces, axis=0), source, axis=0)
+    features = features.reshape(tp_count * group * rows, 3, slab_width)
 
     total_rows = features.shape[0]
     feature_flat = features.reshape(total_rows, 3 * slab_width)

time: 175 us -> 167 us (0.954)
  waiting for transfers between devices: 117 us -> 70.3 us
  starting transfers between devices: 5.44 us -> 36 us
  local copies, waits for them, and re-layouts: 5.65 us -> 12.1 us
  other arithmetic: 5.65 us -> 7.93 us
  matrix products: 17.6 us -> 15.6 us
    all_gather x1 -> x0, waiting for transfers between devices: 57.1 us -> none  [body(): features = lax.all_gather(mine, 'tp', axis=0, tiled=True)]
    ppermute x3 -> x6, starting transfers between devices: 4.57 us -> 35.2 us  [xor_exchange(): yield lax.ppermute(chunk_of(k), axis, perm)]
    ppermute x3 -> x6, waiting for transfers between devices: 4.92 us -> 21.1 us  [xor_exchange(): yield lax.ppermute(chunk_of(k), axis, perm)]
    all_gather x1, waiting for transfers between devices: 17 us -> 13.3 us  [body(): hidden_grads_all = lax.all_gather(hidden_grads, 'rep', axis=0, tiled=True)]
    gather x0 -> x2, local copies, waits for them, and re-layouts: none -> 3.4 us  [body(): features = jnp.take(jnp.stack(pieces, axis=0), source, axis=0)]
    dot_general x1, matrix products: 9.79 us -> 7.79 us  [body(): jnp.dot(feature_flat, fc_block, preferred_element_type=jnp.float32)]
    dot_general x0 -> x1, local copies, waits for them, and re-layouts: none -> 1.78 us  [body(): lax.dot_general(feature_flat, hidden_grads_all, (((0,), (0,)), ((), ())),...]
  transfers between devices with their start and end apart: 8 -> 10, of which waited for: 6 -> 8; matrix products, arithmetic and copies ran while one was open for 2% -> 5% of each run, Pallas kernels for 0% -> 0%
where the time goes in v2:
time: 167 us; the launch traced here: 166 us
  waiting for transfers between devices  70.3 us (42%)
  starting transfers between devices  36 us (22%)
  matrix products  15.6 us (9%)
  between operations  14.4 us (9%)
  local copies, waits for them, and re-layouts  12.1 us (7%)
  blocking collectives  9.93 us (6%)
  other arithmetic  7.93 us (5%)
    ppermute x6, starting transfers between devices, xor_exchange(): yield lax.ppermute(chunk_of(k), axis, perm)  35.2 us
    reduce_scatter x1, waiting for transfers between devices, body(): lax.psum_scatter(jnp.dot(feature_flat, fc_block, preferred_element_type=j...  34.5 us
    ppermute x6, waiting for transfers between devices, xor_exchange(): yield lax.ppermute(chunk_of(k), axis, perm)  21.1 us
    all_gather x1, waiting for transfers between devices, body(): hidden_grads_all = lax.all_gather(hidden_grads, 'rep', axis=0, tiled=True)  13.3 us
    psum x1, blocking collectives, body(): squares = lax.psum(jnp.sum(hidden * hidden, axis=1), 'tp')  9.93 us
    dot_general x1, matrix products, body(): lax.dot_general(feature_flat, hidden_grads_all, (((0,), (0,)), ((), ())),...  7.8 us
    dot_general x1, matrix products, body(): jnp.dot(feature_flat, fc_block, preferred_element_type=jnp.float32)  7.79 us
    gather x2, local copies, waits for them, and re-layouts, body(): features = jnp.take(jnp.stack(pieces, axis=0), source, axis=0)  3.4 us
  transfers between devices with their start and end apart: 10, of which 8 were waited for; matrix products, arithmetic and copies ran while one was open for 5% of the time, Pallas kernels for 0%

profile of v2, /device:TPU:0, one launch (start us, length us, event | category | flops | bytes accessed | tf_op | source)
XLA Modules:
  0.0 166.3 jit_solution(7147263018031063628)
XLA Ops:
  7.2 0.0 copy-start
  7.2 0.0 reduce-scatter.2.cloned.1.call-start
  7.3 0.7 compare_and_fusion
  8.0 0.7 compare_select_fusion
  8.7 0.0 copy-done
  8.7 0.9 gather_fusion
  9.5 0.0 copy-start.1
  9.6 0.0 copy-start.2
  9.6 0.1 bitcast_select_fusion
  9.7 3.0 %collective-permute-start = (bf16[32,2048]{1,0:T(8,128)(2,1)S(1)}, bf16[32,2048]{1,0:T(8,128)(2,1)S(1)}, u32[]{:S(2)}, u32[]{:S(2)}) collective-permute-start(bf16[32,2048]{1,0:T(8,128)(2,1)S(1)} %get-tuple-element.31), channel_id=1, source_target_pairs={{0,1},{1,0},{2,3},{3,2},{4,5},{5,4},{6,7},{7,6},{8,9},{9,8},{10,11... | collective-permute-start | bytes 393224 | tf_op jit(solution)/shard_map/ppermute | solution.py:15
  12.8 1.5 collective-permute-start.2
  14.3 0.1 collective-permute-start.1
  14.3 0.0 copy-done.1
  14.3 0.6 gather_fusion.4
  15.0 0.0 copy-done.2
  15.0 0.0 copy-start.3
  15.0 0.7 gather_fusion.3
  15.7 0.1 broadcast_select_fusion.1
  15.8 0.1 stack.34
  15.8 0.1 stack.33
  16.1 0.1 broadcast_in_dim.81
  16.1 0.1 broadcast_in_dim.82
  16.2 0.0 copy-done.3
  16.2 0.6 gather_fusion.5
  16.9 0.0 collective-permute-done
  16.9 3.5 %collective-permute-done.2 = bf16[32,2048]{1,0:T(8,128)(2,1)S(1)} collective-permute-done((bf16[32,2048]{1,0:T(8,128)(2,1)S(1)}, bf16[32,2048]{1,0:T(8,128)(2,1)S(1)}, u32[]{:S(2)}, u32[]{:S(2)}) %collective-permute-start.2) | collective-permute-done | bytes 131104 | tf_op jit(solution)/shard_map/ppermute | solution.py:15
  20.4 1.4 collective-permute-done.1
  21.8 0.1 add_convert_fusion
  21.9 0.1 stack.35
  22.0 0.7 collective-permute-start.3
  22.7 0.1 collective-permute-start.4
  22.8 0.0 collective-permute-done.3
  22.8 1.4 collective-permute-done.4
  24.3 0.6 gather_fusion.1
  24.9 0.1 bitcast_select_fusion.1
  25.0 15.8 %collective-permute-start.7 = (bf16[64,3,1024]{2,0,1:T(8,128)(2,1)S(1)}, bf16[64,3,1024]{2,0,1:T(8,128)(2,1)S(1)}, u32[]{:S(2)}, u32[]{:S(2)}) collective-permute-start(bf16[64,3,1024]{2,0,1:T(8,128)(2,1)S(1)} %bitcast_select_fusion.1), channel_id=1, source_target_pairs={{0,3},{1,2},{2,1},{3,0},{4,7},{5,6},{6,5},{7,4},{8,11},{9,10},{10,... | collective-permute-start | bytes 1179656 | tf_op jit(solution)/shard_map/ppermute | solution.py:15
  40.8 14.8 %collective-permute-start.6 = (bf16[64,3,1024]{2,0,1:T(8,128)(2,1)S(1)}, bf16[64,3,1024]{2,0,1:T(8,128)(2,1)S(1)}, u32[]{:S(2)}, u32[]{:S(2)}) collective-permute-start(bf16[64,3,1024]{2,0,1:T(8,128)(2,1)S(1)} %bitcast_select_fusion.1), channel_id=1, source_target_pairs={{0,2},{1,3},{2,0},{3,1},{4,6},{5,7},{6,4},{7,5},{8,10},{9,11},{10,... | collective-permute-start | bytes 1179656 | tf_op jit(solution)/shard_map/ppermute | solution.py:15
  55.6 0.0 collective-permute-start.5
  55.6 0.1 bitcast_select_fusion.2
  55.7 2.4 %collective-permute-done.7 = bf16[64,3,1024]{2,0,1:T(8,128)(2,1)S(1)} collective-permute-done((bf16[64,3,1024]{2,0,1:T(8,128)(2,1)S(1)}, bf16[64,3,1024]{2,0,1:T(8,128)(2,1)S(1)}, u32[]{:S(2)}, u32[]{:S(2)}) %collective-permute-start.7) | collective-permute-done | bytes 393248 | tf_op jit(solution)/shard_map/ppermute | solution.py:15
  58.1 12.7 %collective-permute-done.6 = bf16[64,3,1024]{2,0,1:T(8,128)(2,1)S(1)} collective-permute-done((bf16[64,3,1024]{2,0,1:T(8,128)(2,1)S(1)}, bf16[64,3,1024]{2,0,1:T(8,128)(2,1)S(1)}, u32[]{:S(2)}, u32[]{:S(2)}) %collective-permute-start.6) | collective-permute-done | bytes 393248 | tf_op jit(solution)/shard_map/ppermute | solution.py:15
  70.9 1.1 collective-permute-done.5
  71.9 1.3 pad_maximum_fusion
  73.3 2.1 %gather_fusion.2 = bf16[4,64,3,1024]{3,1,2,0:T(8,128)(2,1)S(1)} fusion(bf16[4,64,3,1024]{3,1,2,0:T(8,128)(2,1)} %pad_maximum_fusion, s32[1024]{0:T(1024)S(1)} %pad_clamp_fusion), kind=kCustom, calls=%fused_computation.5 | custom fusion | bytes 3145744 | tf_op jit(solution)/shard_map/jit(_take)/gather | solution.py:54
  75.3 0.2 broadcast_select_fusion
  75.6 1.4 copy.26
  76.9 0.8 copy.30
  77.7 7.8 %fusion.7 = f32[256,2048]{1,0:T(8,128)} fusion(bf16[256,3072]{1,0:T(8,128)(2,1)S(1)} %bitcast.49, bf16[3072,2048]{1,0:T(8,128)(2,1)} %bitcast.55), kind=kOutput, calls=%fused_computation.56 | convolution fusion | flops 3221225472 | bytes 16252928 | tf_op jit(solution)/shard_map/dot_general | solution.py:61
  85.5 0.0 reduce-scatter.2.cloned.1.call-update
  85.5 0.0 all-gather.2.cloned.1.call-start
  85.5 34.5 %reduce-scatter.2.cloned.1.call-done = f32[32,2048]{1,0:T(8,128)} async-done(((f32[256,2048]{1,0:T(8,128)}), f32[32,2048]{1,0:T(8,128)}) %reduce-scatter.2.cloned.1.call-update) | async-done | bytes 262160 | tf_op jit(solution)/shard_map/reduce_scatter | solution.py:60
  120.0 0.0 copy-done.4
  120.0 1.1 multiply_reduce_fusion
  121.1 9.9 %all-reduce = (f32[32]{0:T(128)S(1)}, f32[32]{0:T(128)S(1)}) all-reduce(f32[32]{0:T(128)S(1)} %get-tuple-element.28, f32[32]{0:T(128)S(1)} %get-tuple-element.27), channel_id=1, replica_groups=mesh['rep'=8,'tp'=4] {'tp'}, use_global_device_ids=true, to_apply=%region_2.6 | all-reduce | flops 64 | bytes 512 | tf_op jit(solution)/shard_map/psum | solution.py:66
  131.1 1.8 %subtract_convert_fusion = (bf16[32,2048]{1,0:T(8,128)(2,1)}, bf16[32,2048]{1,0:T(8,128)(2,1)}) fusion(f32[32,2048]{1,0:T(8,128)} %reduce-scatter.2.cloned.1.call-done, bf16[32,2048]{1,0:T(8,128)(2,1)S(1)} %copy-done.4, f32[32]{0:T(128)S(1)} %get-tuple-element.38, f32[2048]{0:T(1024)S(1)} %copy-done.5, f32[32]{0:T(128)S(1)} %get-tuple-element.39), kind=kLoop, calls=%fused_computation.15 | loop fusion | flops 589824 | bytes 663808 | tf_op jit(solution)/shard_map/convert_element_type | solution.py:73
  132.9 0.0 all-gather.2.cloned.1.call-update
  132.9 0.1 broadcast_in_dim.91
  133.0 0.1 broadcast_in_dim.92
  133.0 1.4 copy.27
  134.4 0.8 copy.31
  135.2 1.4 select_bitcast_fusion
  136.5 1.8 %copy.28 = bf16[3072,256]{1,0:T(8,128)(2,1)S(1)} copy(bf16[3072,256]{0,1:T(8,128)(2,1)} %select_bitcast_fusion) | data formatting | bytes 3145728 | tf_op jit(solution)/shard_map/dot_general | solution.py:75
  138.3 13.3 %all-gather.2.cloned.1.call-done = bf16[256,2048]{1,0:T(8,128)(2,1)} async-done(((bf16[32,2048]{1,0:T(8,128)(2,1)}), bf16[256,2048]{1,0:T(8,128)(2,1)}) %all-gather.2.cloned.1.call-update) | async-done | bytes 1048592 | tf_op jit(solution)/shard_map/all_gather | solution.py:74
  151.6 7.8 %convolution_convert_fusion = bf16[3,1024,2048]{2,1,0:T(8,128)(2,1)} fusion(bf16[3,1024,256]{2,1,0:T(8,128)(2,1)S(1)} %bitcast.44, bf16[256,2048]{1,0:T(8,128)(2,1)} %all-gather.2.cloned.1.call-done), kind=kOutput, calls=%fused_computation.6 | convolution fusion | flops 3227516928 | bytes 15204352 | tf_op jit(solution)/shard_map/dot_general | solution.py:75
  (18 shorter events, 0.3 us)
Async XLA Ops:
  7.2 1.5 copy-start
  7.2 112.8 %reduce-scatter.2.cloned.1.call-start = ((), (), s32[]{:S(2)}) async-start(), calls=%async_computation.1 | async-start | bytes 2359296 | tf_op jit(solution)/shard_map/reduce_scatter | solution.py:60
  9.5 4.8 %copy-start.1 = (bf16[64,2048]{1,0:T(8,128)(2,1)S(1)}, bf16[64,2048]{1,0:T(8,128)(2,1)}, u32[]{:S(2)}) copy-start(bf16[64,2048]{1,0:T(8,128)(2,1)} %param.17) | copy-start | bytes 786436
  9.6 5.4 %copy-start.2 = (bf16[64,2048]{1,0:T(8,128)(2,1)S(1)}, bf16[64,2048]{1,0:T(8,128)(2,1)}, u32[]{:S(2)}) copy-start(bf16[64,2048]{1,0:T(8,128)(2,1)} %param.16) | copy-start | bytes 786436
  9.7 7.2 %collective-permute-start = (bf16[32,2048]{1,0:T(8,128)(2,1)S(1)}, bf16[32,2048]{1,0:T(8,128)(2,1)S(1)}, u32[]{:S(2)}, u32[]{:S(2)}) collective-permute-start(bf16[32,2048]{1,0:T(8,128)(2,1)S(1)} %get-tuple-element.31), channel_id=1, source_target_pairs={{0,1},{1,0},{2,3},{3,2},{4,5},{5,4},{6,7},{7,6},{8,9},{9,8},{10,11... | collective-permute-start | bytes 393224 | tf_op jit(solution)/shard_map/ppermute | solution.py:15
  12.8 7.6 %collective-permute-start.2 = (bf16[32,2048]{1,0:T(8,128)(2,1)S(1)}, bf16[32,2048]{1,0:T(8,128)(2,1)S(1)}, u32[]{:S(2)}, u32[]{:S(2)}) collective-permute-start(bf16[32,2048]{1,0:T(8,128)(2,1)S(1)} %get-tuple-element.32), channel_id=1, source_target_pairs={{0,3},{1,2},{2,1},{3,0},{4,7},{5,6},{6,5},{7,4},{8,11},{9,10},{10,... | collective-permute-start | bytes 393224 | tf_op jit(solution)/shard_map/ppermute | solution.py:15
  14.3 7.5 %collective-permute-start.1 = (bf16[32,2048]{1,0:T(8,128)(2,1)S(1)}, bf16[32,2048]{1,0:T(8,128)(2,1)S(1)}, u32[]{:S(2)}, u32[]{:S(2)}) collective-permute-start(bf16[32,2048]{1,0:T(8,128)(2,1)S(1)} %get-tuple-element.33), channel_id=1, source_target_pairs={{0,2},{1,3},{2,0},{3,1},{4,6},{5,7},{6,4},{7,5},{8,10},{9,11},{10,... | collective-permute-start | bytes 393224 | tf_op jit(solution)/shard_map/ppermute | solution.py:15
  15.0 1.2 copy-start.3
  22.0 0.8 collective-permute-start.3
  22.7 1.5 collective-permute-start.4
  25.0 33.1 %collective-permute-start.7 = (bf16[64,3,1024]{2,0,1:T(8,128)(2,1)S(1)}, bf16[64,3,1024]{2,0,1:T(8,128)(2,1)S(1)}, u32[]{:S(2)}, u32[]{:S(2)}) collective-permute-start(bf16[64,3,1024]{2,0,1:T(8,128)(2,1)S(1)} %bitcast_select_fusion.1), channel_id=1, source_target_pairs={{0,3},{1,2},{2,1},{3,0},{4,7},{5,6},{6,5},{7,4},{8,11},{9,10},{10,... | collective-permute-start | bytes 1179656 | tf_op jit(solution)/shard_map/ppermute | solution.py:15
  40.8 30.0 %collective-permute-start.6 = (bf16[64,3,1024]{2,0,1:T(8,128)(2,1)S(1)}, bf16[64,3,1024]{2,0,1:T(8,128)(2,1)S(1)}, u32[]{:S(2)}, u32[]{:S(2)}) collective-permute-start(bf16[64,3,1024]{2,0,1:T(8,128)(2,1)S(1)} %bitcast_select_fusion.1), channel_id=1, source_target_pairs={{0,2},{1,3},{2,0},{3,1},{4,6},{5,7},{6,4},{7,5},{8,10},{9,11},{10,... | collective-permute-start | bytes 1179656 | tf_op jit(solution)/shard_map/ppermute | solution.py:15
  55.6 16.3 %collective-permute-start.5 = (bf16[64,3,1024]{2,0,1:T(8,128)(2,1)S(1)}, bf16[64,3,1024]{2,0,1:T(8,128)(2,1)S(1)}, u32[]{:S(2)}, u32[]{:S(2)}) collective-permute-start(bf16[64,3,1024]{2,0,1:T(8,128)(2,1)S(1)} %bitcast_select_fusion.1), channel_id=1, source_target_pairs={{0,1},{1,0},{2,3},{3,2},{4,5},{5,4},{6,7},{7,6},{8,9},{9,8},{10,11... | collective-permute-start | bytes 1179656 | tf_op jit(solution)/shard_map/ppermute | solution.py:15
  85.5 34.6 %copy-start.4 = (bf16[32,2048]{1,0:T(8,128)(2,1)S(1)}, bf16[32,2048]{1,0:T(8,128)(2,1)}, u32[]{:S(2)}) copy-start(bf16[32,2048]{1,0:T(8,128)(2,1)} %param.21) | copy-start | bytes 393220
  85.5 34.6 %copy-start.5 = (f32[2048]{0:T(1024)S(1)}, f32[2048]{0:T(1024)}, u32[]{:S(2)}) copy-start(f32[2048]{0:T(1024)} %param.20) | copy-start | bytes 24580
  85.5 66.1 %all-gather.2.cloned.1.call-start = ((), (), s32[]{:S(2)}) async-start(), calls=%async_computation.2 | async-start | bytes 1179648 | tf_op jit(solution)/shard_map/all_gather | solution.py:74
Sparse Core Ops, SparseCore 0:
  85.6 34.3 reduce-scatter.1
  133.0 18.5 all-gather.1

commit v3 on v2

--- a/solution.py
+++ b/solution.py
@@ -57,17 +57,29 @@
     total_rows = features.shape[0]
     feature_flat = features.reshape(total_rows, 3 * slab_width)
     fc_block = fc_weight.reshape(3 * slab_width, fc_weight.shape[2])
-    hidden = lax.psum_scatter(
-        jnp.dot(feature_flat, fc_block, preferred_element_type=jnp.float32),
-        "rep",
-        scatter_dimension=0,
-        tiled=True,
+    projected = jnp.dot(feature_flat, fc_block, preferred_element_type=jnp.float32)
+
+    parity = rep_index % 2
+    chip = rep_index // 2
+    by_chip = projected.reshape(rep_count // 2, 2, rows, projected.shape[1])
+    own_parity = jnp.take(by_chip, parity, axis=1)
+    other_parity = jnp.take(by_chip, 1 - parity, axis=1)
+    chip_sum = own_parity + lax.ppermute(
+        other_parity, "rep", [(i, i ^ 1) for i in range(rep_count)]
     )
-    squares = lax.psum(jnp.sum(hidden * hidden, axis=1), "tp")
+    hidden = jnp.take(chip_sum, chip, axis=0)
+    for k in range(1, rep_count // 2):
+        block = jnp.take(chip_sum, chip ^ k, axis=0).astype(jnp.bfloat16)
+        got = lax.ppermute(block, "rep", [(i, i ^ (2 * k)) for i in range(rep_count)])
+        hidden = hidden + got.astype(jnp.float32)
+
+    scaled = grad_normed.astype(jnp.float32) * norm_gain
+    stats = jnp.stack([jnp.sum(hidden * hidden, axis=1), jnp.sum(scaled * hidden, axis=1)])
+    gathered = jnp.stack([stats] + list(xor_exchange(lambda k: stats, "tp", tp_count)))
+    stats = jnp.sum(jnp.take(gathered, tp_index ^ jnp.arange(tp_count, dtype=jnp.int32), axis=0), axis=0)
+    squares, inner_sum = stats[0], stats[1]
     inv_rms = lax.rsqrt(squares / D + EPSILON)
     normed = (hidden * inv_rms[:, None] * norm_gain).astype(jnp.bfloat16)
-    scaled = grad_normed.astype(jnp.float32) * norm_gain
-    inner_sum = lax.psum(jnp.sum(scaled * hidden, axis=1), "tp")
     hidden_grads = (
         inv_rms[:, None] * scaled - hidden * (inv_rms**3 * inner_sum / D)[:, None]
     ).astype(jnp.bfloat16)

time: 167 us -> 160 us (0.958)
  waiting for transfers between devices: 70.3 us -> 56.2 us
  blocking collectives: 9.93 us -> 0 us
  local copies, waits for them, and re-layouts: 12.1 us -> 20.9 us
  starting transfers between devices: 36 us -> 43 us
  other arithmetic: 7.93 us -> 9.95 us
    reduce_scatter x1 -> x0, waiting for transfers between devices: 34.5 us -> none  [body(): lax.psum_scatter(jnp.dot(feature_flat, fc_block, preferred_element_type=j...]
    ppermute x0 -> x4, waiting for transfers between devices: none -> 14.7 us  [the longest x3 11.7 us: body(): got = lax.ppermute(block, 'rep', [(i, i ^ 2 * k) for i in range(rep_count)])]
    psum x1 -> x0, blocking collectives: 9.93 us -> none  [body(): squares = lax.psum(jnp.sum(hidden * hidden, axis=1), 'tp')]
    select_n x1 -> x2, local copies, waits for them, and re-layouts: 1.35 us -> 8.05 us  [body(): features = jnp.take(jnp.stack(pieces, axis=0), source, axis=0)]
    ppermute x6 -> x9, waiting for transfers between devices: 21.1 us -> 25.3 us  [xor_exchange(): yield lax.ppermute(chunk_of(k), axis, perm)]
    ppermute x6 -> x9, starting transfers between devices: 35.2 us -> 38.7 us  [xor_exchange(): yield lax.ppermute(chunk_of(k), axis, perm)]
    ppermute x0 -> x4, starting transfers between devices: none -> 3.55 us  [the longest x3 3.55 us: body(): got = lax.ppermute(block, 'rep', [(i, i ^ 2 * k) for i in range(rep_count)])]
  transfers between devices with their start and end apart: 10 -> 16, of which waited for: 8 -> 14; matrix products, arithmetic and copies ran while one was open for 5% -> 5% of each run, Pallas kernels for 0% -> 0%
where the time goes in v3:
time: 160 us; the launch traced here: 159 us
  waiting for transfers between devices  56.2 us (35%)
  starting transfers between devices  43 us (27%)
  local copies, waits for them, and re-layouts  20.9 us (13%)
  matrix products  14.7 us (9%)
  between operations  14.4 us (9%)
  other arithmetic  9.95 us (6%)
    ppermute x9, starting transfers between devices, xor_exchange(): yield lax.ppermute(chunk_of(k), axis, perm)  38.7 us
    ppermute x9, waiting for transfers between devices, xor_exchange(): yield lax.ppermute(chunk_of(k), axis, perm)  25.3 us
    all_gather x1, waiting for transfers between devices, body(): hidden_grads_all = lax.all_gather(hidden_grads, 'rep', axis=0, tiled=True)  14.8 us
    ppermute x3, waiting for transfers between devices, body(): got = lax.ppermute(block, 'rep', [(i, i ^ 2 * k) for i in range(rep_count)])  11.7 us
    select_n x2, local copies, waits for them, and re-layouts, body(): features = jnp.take(jnp.stack(pieces, axis=0), source, axis=0)  8.05 us
    dot_general x1, matrix products, body(): lax.dot_general(feature_flat, hidden_grads_all, (((0,), (0,)), ((), ())),...  7.8 us
    dot_general x1, matrix products, body(): jnp.dot(feature_flat, fc_block, preferred_element_type=jnp.float32)  6.86 us
    ppermute x3, starting transfers between devices, body(): got = lax.ppermute(block, 'rep', [(i, i ^ 2 * k) for i in range(rep_count)])  3.55 us
  transfers between devices with their start and end apart: 16, of which 14 were waited for; matrix products, arithmetic and copies ran while one was open for 5% of the time, Pallas kernels for 0%

profile of v3, /device:TPU:0, one launch (start us, length us, event | category | flops | bytes accessed | tf_op | source)
XLA Modules:
  0.0 159.1 jit_solution(15603499222340668111)
XLA Ops:
  7.3 0.7 compare_and_fusion
  8.0 0.7 compare_select_fusion
  8.7 0.9 gather_fusion
  9.6 0.1 bitcast_select_fusion.1
  9.7 3.0 %collective-permute-start = (bf16[32,2048]{1,0:T(8,128)(2,1)S(1)}, bf16[32,2048]{1,0:T(8,128)(2,1)S(1)}, u32[]{:S(2)}, u32[]{:S(2)}) collective-permute-start(bf16[32,2048]{1,0:T(8,128)(2,1)S(1)} %get-tuple-element.57), channel_id=1, source_target_pairs={{0,1},{1,0},{2,3},{3,2},{4,5},{5,4},{6,7},{7,6},{8,9},{9,8},{10,11... | collective-permute-start | bytes 393224 | tf_op jit(solution)/shard_map/ppermute | solution.py:15
  12.8 1.5 collective-permute-start.2
  14.3 0.6 gather_fusion.5
  15.0 0.7 gather_fusion.4
  15.7 0.1 broadcast_select_fusion.1
  15.8 0.1 stack.58
  15.8 0.1 stack.57
  16.1 0.1 broadcast_in_dim.109
  16.1 0.1 broadcast_in_dim.110
  16.2 0.6 gather_fusion.6
  16.9 3.5 %collective-permute-done.2 = bf16[32,2048]{1,0:T(8,128)(2,1)S(1)} collective-permute-done((bf16[32,2048]{1,0:T(8,128)(2,1)S(1)}, bf16[32,2048]{1,0:T(8,128)(2,1)S(1)}, u32[]{:S(2)}, u32[]{:S(2)}) %collective-permute-start.2) | collective-permute-done | bytes 131104 | tf_op jit(solution)/shard_map/ppermute | solution.py:15
  20.4 1.4 collective-permute-done.1
  21.8 0.1 add_convert_fusion
  21.9 0.1 stack.59
  22.0 0.7 collective-permute-start.3
  22.7 0.1 collective-permute-start.4
  22.8 1.4 collective-permute-done.4
  24.3 0.6 gather_fusion.1
  24.9 0.1 bitcast_select_fusion.2
  25.0 15.8 %collective-permute-start.7 = (bf16[64,3,1024]{2,0,1:T(8,128)(2,1)S(1)}, bf16[64,3,1024]{2,0,1:T(8,128)(2,1)S(1)}, u32[]{:S(2)}, u32[]{:S(2)}) collective-permute-start(bf16[64,3,1024]{2,0,1:T(8,128)(2,1)S(1)} %bitcast_select_fusion.2), channel_id=1, source_target_pairs={{0,3},{1,2},{2,1},{3,0},{4,7},{5,6},{6,5},{7,4},{8,11},{9,10},{10,... | collective-permute-start | bytes 1179656 | tf_op jit(solution)/shard_map/ppermute | solution.py:15
  40.8 14.8 %collective-permute-start.6 = (bf16[64,3,1024]{2,0,1:T(8,128)(2,1)S(1)}, bf16[64,3,1024]{2,0,1:T(8,128)(2,1)S(1)}, u32[]{:S(2)}, u32[]{:S(2)}) collective-permute-start(bf16[64,3,1024]{2,0,1:T(8,128)(2,1)S(1)} %bitcast_select_fusion.2), channel_id=1, source_target_pairs={{0,2},{1,3},{2,0},{3,1},{4,6},{5,7},{6,4},{7,5},{8,10},{9,11},{10,... | collective-permute-start | bytes 1179656 | tf_op jit(solution)/shard_map/ppermute | solution.py:15
  55.6 0.1 bitcast_select_fusion.3
  55.7 2.4 %collective-permute-done.7 = bf16[64,3,1024]{2,0,1:T(8,128)(2,1)S(1)} collective-permute-done((bf16[64,3,1024]{2,0,1:T(8,128)(2,1)S(1)}, bf16[64,3,1024]{2,0,1:T(8,128)(2,1)S(1)}, u32[]{:S(2)}, u32[]{:S(2)}) %collective-permute-start.7) | collective-permute-done | bytes 393248 | tf_op jit(solution)/shard_map/ppermute | solution.py:15
  58.1 12.7 %collective-permute-done.6 = bf16[64,3,1024]{2,0,1:T(8,128)(2,1)S(1)} collective-permute-done((bf16[64,3,1024]{2,0,1:T(8,128)(2,1)S(1)}, bf16[64,3,1024]{2,0,1:T(8,128)(2,1)S(1)}, u32[]{:S(2)}, u32[]{:S(2)}) %collective-permute-start.6) | collective-permute-done | bytes 393248 | tf_op jit(solution)/shard_map/ppermute | solution.py:15
  70.9 1.1 collective-permute-done.5
  71.9 1.3 pad_maximum_fusion
  73.3 2.1 %gather_fusion.2 = bf16[4,64,3,1024]{3,1,2,0:T(8,128)(2,1)S(1)} fusion(bf16[4,64,3,1024]{3,1,2,0:T(8,128)(2,1)} %pad_maximum_fusion, s32[1024]{0:T(1024)S(1)} %pad_clamp_fusion), kind=kCustom, calls=%fused_computation.5 | custom fusion | bytes 3145744 | tf_op jit(solution)/shard_map/jit(_take)/gather | solution.py:54
  75.3 0.2 broadcast_select_fusion
  75.6 2.7 %copy.29 = bf16[4,64,3,1024]{3,2,1,0:T(4,128)(2,1)} copy(bf16[4,64,3,1024]{3,1,2,0:T(8,128)(2,1)S(1)} %broadcast_select_fusion) | data formatting | bytes 3145728 | tf_op jit(solution)/shard_map/jit(_take)/select_n | solution.py:54
  78.2 5.4 %select_n.158 = bf16[4,2,32,3072]{3,2,1,0:T(8,128)(2,1)} reshape(bf16[4,64,3,1024]{3,2,1,0:T(4,128)(2,1)} %copy.29) | data formatting | bytes 3145728 | tf_op jit(solution)/shard_map/jit(_take)/select_n | solution.py:54
  83.6 6.9 %fusion.13 = f32[4,2,32,2048]{3,2,1,0:T(8,128)S(1)} fusion(bf16[4,2,32,3072]{3,2,1,0:T(8,128)(2,1)} %select_n.158, bf16[3072,2048,1,1]{1,0,3,2:T(8,128)(2,1)} %bitcast.99), kind=kOutput, calls=%fused_computation.71 | convolution fusion | flops 3221225472 | bytes 16252928 | tf_op jit(solution)/shard_map/dot_general | solution.py:60
  90.5 1.3 copy-done.5
  91.8 1.1 select_bitcast_fusion.1
  92.9 3.0 %collective-permute-done.8 = f32[4,32,2048]{2,1,0:T(8,128)} collective-permute-done((f32[4,32,2048]{2,1,0:T(8,128)}, f32[4,32,2048]{2,1,0:T(8,128)}, u32[]{:S(2)}, u32[]{:S(2)}) %collective-permute-start.8) | collective-permute-done | bytes 1048608 | tf_op jit(solution)/shard_map/ppermute | solution.py:67
  95.9 1.7 %fusion.1 = f32[4,32,2048]{2,1,0:T(8,128)S(1)} fusion(f32[4,32,2048]{2,1,0:T(8,128)} %collective-permute-done.8, f32[4,2,32,2048]{3,2,1,0:T(8,128)} %copy-done.5, s32[]{:T(128)S(6)} %select_n.220, pred[]{:T(512)S(6)} %and.116), kind=kLoop, calls=%fused_computation.13 | loop fusion | flops 524288 | bytes 3145733 | tf_op jit(solution)/shard_map/add | solution.py:67
  97.5 1.0 copy-done.4
  98.6 0.1 collective-permute-start.9
  98.6 2.2 %collective-permute-start.11 = (bf16[32,2048]{1,0:T(8,128)(2,1)S(1)}, bf16[32,2048]{1,0:T(8,128)(2,1)S(1)}, u32[]{:S(2)}, u32[]{:S(2)}) collective-permute-start(bf16[32,2048]{1,0:T(8,128)(2,1)S(1)} %get-tuple-element.55), channel_id=1, source_target_pairs={{0,24},{4,28},{8,16},{12,20},{16,8},{20,12},{24,0},{28,4},{1,25},{... | collective-permute-start | bytes 393224 | tf_op jit(solution)/shard_map/ppermute | solution.py:73
  100.8 1.3 collective-permute-start.10
  102.1 2.0 %collective-permute-done.9 = bf16[32,2048]{1,0:T(8,128)(2,1)S(1)} collective-permute-done((bf16[32,2048]{1,0:T(8,128)(2,1)S(1)}, bf16[32,2048]{1,0:T(8,128)(2,1)S(1)}, u32[]{:S(2)}, u32[]{:S(2)}) %collective-permute-start.9) | collective-permute-done | bytes 131104 | tf_op jit(solution)/shard_map/ppermute | solution.py:73
  104.2 3.8 %collective-permute-done.11 = bf16[32,2048]{1,0:T(8,128)(2,1)S(1)} collective-permute-done((bf16[32,2048]{1,0:T(8,128)(2,1)S(1)}, bf16[32,2048]{1,0:T(8,128)(2,1)S(1)}, u32[]{:S(2)}, u32[]{:S(2)}) %collective-permute-start.11) | collective-permute-done | bytes 131104 | tf_op jit(solution)/shard_map/ppermute | solution.py:73
  108.0 5.8 %collective-permute-done.10 = bf16[32,2048]{1,0:T(8,128)(2,1)S(1)} collective-permute-done((bf16[32,2048]{1,0:T(8,128)(2,1)S(1)}, bf16[32,2048]{1,0:T(8,128)(2,1)S(1)}, u32[]{:S(2)}, u32[]{:S(2)}) %collective-permute-start.10) | collective-permute-done | bytes 131104 | tf_op jit(solution)/shard_map/ppermute | solution.py:73
  113.8 1.2 multiply_reduce_fusion.1
  115.0 1.5 collective-permute-start.13
  116.4 1.8 %collective-permute-start.12 = (f32[2,32]{1,0:T(2,128)S(1)}, f32[2,32]{1,0:T(2,128)S(1)}, u32[]{:S(2)}, u32[]{:S(2)}) collective-permute-start(f32[2,32]{1,0:T(2,128)S(1)} %get-tuple-element.65), channel_id=1, source_target_pairs={{0,1},{1,0},{2,3},{3,2},{4,5},{5,4},{6,7},{7,6},{8,9},{9,8},{10,11... | collective-permute-start | bytes 776 | tf_op jit(solution)/shard_map/ppermute | solution.py:15
  118.2 0.3 collective-permute-start.14
  118.5 0.1 collective-permute-done.13
  118.6 1.4 collective-permute-done.12
  120.0 2.7 %collective-permute-done.14 = f32[2,32]{1,0:T(2,128)S(1)} collective-permute-done((f32[2,32]{1,0:T(2,128)S(1)}, f32[2,32]{1,0:T(2,128)S(1)}, u32[]{:S(2)}, u32[]{:S(2)}) %collective-permute-start.14) | collective-permute-done | bytes 288 | tf_op jit(solution)/shard_map/ppermute | solution.py:15
  122.7 0.6 gather_fusion.3
  123.3 0.1 select_reduce_fusion
  123.4 0.9 subtract_convert_fusion
  124.3 0.1 broadcast_in_dim.121
  124.3 0.1 broadcast_in_dim.122
  124.4 1.4 copy.31
  125.8 0.8 copy.36
  126.5 1.4 select_bitcast_fusion
  127.9 1.7 %copy.32 = bf16[3072,256]{1,0:T(8,128)(2,1)S(1)} copy(bf16[3072,256]{0,1:T(8,128)(2,1)} %select_bitcast_fusion) | data formatting | bytes 3145728 | tf_op jit(solution)/shard_map/dot_general | solution.py:87
  129.6 14.8 %all-gather.2.cloned.1.call-done = bf16[256,2048]{1,0:T(8,128)(2,1)} async-done(((bf16[32,2048]{1,0:T(8,128)(2,1)}), bf16[256,2048]{1,0:T(8,128)(2,1)}) %all-gather.2.cloned.1.call-update) | async-done | bytes 1048592 | tf_op jit(solution)/shard_map/all_gather | solution.py:86
  144.5 7.8 %convolution_convert_fusion = bf16[3,1024,2048]{2,1,0:T(8,128)(2,1)} fusion(bf16[3,1024,256]{2,1,0:T(8,128)(2,1)S(1)} %bitcast.85, bf16[256,2048]{1,0:T(8,128)(2,1)} %all-gather.2.cloned.1.call-done), kind=kOutput, calls=%fused_computation.7 | convolution fusion | flops 3227516928 | bytes 15204352 | tf_op jit(solution)/shard_map/dot_general | solution.py:87
  (40 shorter events, 0.5 us)
Async XLA Ops:
  7.2 1.5 copy-start
  7.2 137.3 %all-gather.2.cloned.1.call-start = ((), (), s32[]{:S(2)}) async-start(), calls=%async_computation | async-start | bytes 1179648 | tf_op jit(solution)/shard_map/all_gather | solution.py:86
  9.5 4.8 %copy-start.1 = (bf16[64,2048]{1,0:T(8,128)(2,1)S(1)}, bf16[64,2048]{1,0:T(8,128)(2,1)}, u32[]{:S(2)}) copy-start(bf16[64,2048]{1,0:T(8,128)(2,1)} %param.21) | copy-start | bytes 786436
  9.6 5.4 %copy-start.2 = (bf16[64,2048]{1,0:T(8,128)(2,1)S(1)}, bf16[64,2048]{1,0:T(8,128)(2,1)}, u32[]{:S(2)}) copy-start(bf16[64,2048]{1,0:T(8,128)(2,1)} %param.20) | copy-start | bytes 786436
  9.7 7.2 %collective-permute-start = (bf16[32,2048]{1,0:T(8,128)(2,1)S(1)}, bf16[32,2048]{1,0:T(8,128)(2,1)S(1)}, u32[]{:S(2)}, u32[]{:S(2)}) collective-permute-start(bf16[32,2048]{1,0:T(8,128)(2,1)S(1)} %get-tuple-element.57), channel_id=1, source_target_pairs={{0,1},{1,0},{2,3},{3,2},{4,5},{5,4},{6,7},{7,6},{8,9},{9,8},{10,11... | collective-permute-start | bytes 393224 | tf_op jit(solution)/shard_map/ppermute | solution.py:15
  12.8 7.6 %collective-permute-start.2 = (bf16[32,2048]{1,0:T(8,128)(2,1)S(1)}, bf16[32,2048]{1,0:T(8,128)(2,1)S(1)}, u32[]{:S(2)}, u32[]{:S(2)}) collective-permute-start(bf16[32,2048]{1,0:T(8,128)(2,1)S(1)} %get-tuple-element.58), channel_id=1, source_target_pairs={{0,3},{1,2},{2,1},{3,0},{4,7},{5,6},{6,5},{7,4},{8,11},{9,10},{10,... | collective-permute-start | bytes 393224 | tf_op jit(solution)/shard_map/ppermute | solution.py:15
  14.3 7.5 %collective-permute-start.1 = (bf16[32,2048]{1,0:T(8,128)(2,1)S(1)}, bf16[32,2048]{1,0:T(8,128)(2,1)S(1)}, u32[]{:S(2)}, u32[]{:S(2)}) collective-permute-start(bf16[32,2048]{1,0:T(8,128)(2,1)S(1)} %get-tuple-element.59), channel_id=1, source_target_pairs={{0,2},{1,3},{2,0},{3,1},{4,6},{5,7},{6,4},{7,5},{8,10},{9,11},{10,... | collective-permute-start | bytes 393224 | tf_op jit(solution)/shard_map/ppermute | solution.py:15
  15.0 1.2 copy-start.3
  22.0 0.8 collective-permute-start.3
  22.7 1.5 collective-permute-start.4
  25.0 33.1 %collective-permute-start.7 = (bf16[64,3,1024]{2,0,1:T(8,128)(2,1)S(1)}, bf16[64,3,1024]{2,0,1:T(8,128)(2,1)S(1)}, u32[]{:S(2)}, u32[]{:S(2)}) collective-permute-start(bf16[64,3,1024]{2,0,1:T(8,128)(2,1)S(1)} %bitcast_select_fusion.2), channel_id=1, source_target_pairs={{0,3},{1,2},{2,1},{3,0},{4,7},{5,6},{6,5},{7,4},{8,11},{9,10},{10,... | collective-permute-start | bytes 1179656 | tf_op jit(solution)/shard_map/ppermute | solution.py:15
  40.8 30.0 %collective-permute-start.6 = (bf16[64,3,1024]{2,0,1:T(8,128)(2,1)S(1)}, bf16[64,3,1024]{2,0,1:T(8,128)(2,1)S(1)}, u32[]{:S(2)}, u32[]{:S(2)}) collective-permute-start(bf16[64,3,1024]{2,0,1:T(8,128)(2,1)S(1)} %bitcast_select_fusion.2), channel_id=1, source_target_pairs={{0,2},{1,3},{2,0},{3,1},{4,6},{5,7},{6,4},{7,5},{8,10},{9,11},{10,... | collective-permute-start | bytes 1179656 | tf_op jit(solution)/shard_map/ppermute | solution.py:15
  55.6 16.3 %collective-permute-start.5 = (bf16[64,3,1024]{2,0,1:T(8,128)(2,1)S(1)}, bf16[64,3,1024]{2,0,1:T(8,128)(2,1)S(1)}, u32[]{:S(2)}, u32[]{:S(2)}) collective-permute-start(bf16[64,3,1024]{2,0,1:T(8,128)(2,1)S(1)} %bitcast_select_fusion.2), channel_id=1, source_target_pairs={{0,1},{1,0},{2,3},{3,2},{4,5},{5,4},{6,7},{7,6},{8,9},{9,8},{10,11... | collective-permute-start | bytes 1179656 | tf_op jit(solution)/shard_map/ppermute | solution.py:15
  90.5 1.3 copy-start.5
  92.9 3.0 %collective-permute-start.8 = (f32[4,32,2048]{2,1,0:T(8,128)}, f32[4,32,2048]{2,1,0:T(8,128)}, u32[]{:S(2)}, u32[]{:S(2)}) collective-permute-start(f32[4,32,2048]{2,1,0:T(8,128)} %select_bitcast_fusion.1), channel_id=1, source_target_pairs={{0,4},{4,0},{8,12},{12,8},{16,20},{20,16},{24,28},{28,24},{1,5},{5... | collective-permute-start | bytes 3145736 | tf_op jit(solution)/shard_map/ppermute | solution.py:67
  92.9 20.9 %copy-start.6 = (bf16[32,2048]{1,0:T(8,128)(2,1)S(1)}, bf16[32,2048]{1,0:T(8,128)(2,1)}, u32[]{:S(2)}) copy-start(bf16[32,2048]{1,0:T(8,128)(2,1)} %param.25) | copy-start | bytes 393220
  92.9 20.9 %copy-start.7 = (f32[2048]{0:T(1024)S(1)}, f32[2048]{0:T(1024)}, u32[]{:S(2)}) copy-start(f32[2048]{0:T(1024)} %param.24) | copy-start | bytes 24580
  97.5 1.0 copy-start.4
  98.6 5.6 %collective-permute-start.9 = (bf16[32,2048]{1,0:T(8,128)(2,1)S(1)}, bf16[32,2048]{1,0:T(8,128)(2,1)S(1)}, u32[]{:S(2)}, u32[]{:S(2)}) collective-permute-start(bf16[32,2048]{1,0:T(8,128)(2,1)S(1)} %get-tuple-element.54), channel_id=1, source_target_pairs={{0,8},{4,12},{8,0},{12,4},{16,24},{20,28},{24,16},{28,20},{1,9},{5... | collective-permute-start | bytes 393224 | tf_op jit(solution)/shard_map/ppermute | solution.py:73
  98.6 9.3 %collective-permute-start.11 = (bf16[32,2048]{1,0:T(8,128)(2,1)S(1)}, bf16[32,2048]{1,0:T(8,128)(2,1)S(1)}, u32[]{:S(2)}, u32[]{:S(2)}) collective-permute-start(bf16[32,2048]{1,0:T(8,128)(2,1)S(1)} %get-tuple-element.55), channel_id=1, source_target_pairs={{0,24},{4,28},{8,16},{12,20},{16,8},{20,12},{24,0},{28,4},{1,25},{... | collective-permute-start | bytes 393224 | tf_op jit(solution)/shard_map/ppermute | solution.py:73
  100.8 13.0 %collective-permute-start.10 = (bf16[32,2048]{1,0:T(8,128)(2,1)S(1)}, bf16[32,2048]{1,0:T(8,128)(2,1)S(1)}, u32[]{:S(2)}, u32[]{:S(2)}) collective-permute-start(bf16[32,2048]{1,0:T(8,128)(2,1)S(1)} %get-tuple-element.56), channel_id=1, source_target_pairs={{0,16},{4,20},{8,24},{12,28},{16,0},{20,4},{24,8},{28,12},{1,17},{... | collective-permute-start | bytes 393224 | tf_op jit(solution)/shard_map/ppermute | solution.py:73
  115.0 3.6 %collective-permute-start.13 = (f32[2,32]{1,0:T(2,128)S(1)}, f32[2,32]{1,0:T(2,128)S(1)}, u32[]{:S(2)}, u32[]{:S(2)}) collective-permute-start(f32[2,32]{1,0:T(2,128)S(1)} %get-tuple-element.65), channel_id=1, source_target_pairs={{0,2},{1,3},{2,0},{3,1},{4,6},{5,7},{6,4},{7,5},{8,10},{9,11},{10,... | collective-permute-start | bytes 776 | tf_op jit(solution)/shard_map/ppermute | solution.py:15
  116.4 3.6 %collective-permute-start.12 = (f32[2,32]{1,0:T(2,128)S(1)}, f32[2,32]{1,0:T(2,128)S(1)}, u32[]{:S(2)}, u32[]{:S(2)}) collective-permute-start(f32[2,32]{1,0:T(2,128)S(1)} %get-tuple-element.65), channel_id=1, source_target_pairs={{0,1},{1,0},{2,3},{3,2},{4,5},{5,4},{6,7},{7,6},{8,9},{9,8},{10,11... | collective-permute-start | bytes 776 | tf_op jit(solution)/shard_map/ppermute | solution.py:15
  118.2 4.5 %collective-permute-start.14 = (f32[2,32]{1,0:T(2,128)S(1)}, f32[2,32]{1,0:T(2,128)S(1)}, u32[]{:S(2)}, u32[]{:S(2)}) collective-permute-start(f32[2,32]{1,0:T(2,128)S(1)} %get-tuple-element.65), channel_id=1, source_target_pairs={{0,3},{1,2},{2,1},{3,0},{4,7},{5,6},{6,5},{7,4},{8,11},{9,10},{10,... | collective-permute-start | bytes 776 | tf_op jit(solution)/shard_map/ppermute | solution.py:15
Sparse Core Ops, SparseCore 0:
  124.4 20.0 all-gather.1

commit v4 on v3

v4 whole, which is shorter than its diff:
```python
import jax
import jax.numpy as jnp
from jax import lax
from jax.sharding import PartitionSpec as P

D = 8192


EPSILON = 1e-06


def xor_exchange(chunk_of, axis, size):
    for k in range(1, size):
        perm = [(i, i ^ k) for i in range(size)]
        yield lax.ppermute(chunk_of(k), axis, perm)


def pick(x, index, axis):
    return lax.dynamic_index_in_dim(x, index, axis, keepdims=False)


def place(buffer, piece, index):
    return lax.dynamic_update_index_in_dim(buffer, piece, index, 0)


def body(partials, residual, lower, middle, accepted, fc_weight, norm_gain, grad_normed):
    rep_count = lax.axis_size("rep")
    tp_count = lax.axis_size("tp")
    rep_index = lax.axis_index("rep")
    tp_index = lax.axis_index("tp")
    rows = accepted.shape[0]
    tp_width = residual.shape[1]
    parity = rep_index % 2
    chip = rep_index // 2
    chips = rep_count // 2

    picked = jnp.take(partials, accepted, axis=0).reshape(rows, tp_count, tp_width)
    summed = pick(picked, tp_index, 1).astype(jnp.float32)
    for got in xor_exchange(lambda k: pick(picked, tp_index ^ k, 1), "tp", tp_count):
        summed = summed + got.astype(jnp.float32)
    upper_rows = (jnp.take(residual, accepted, axis=0).astype(jnp.float32) + summed).astype(
        jnp.bfloat16
    )
    local_rows = jnp.stack(
        [jnp.take(lower, accepted, axis=0), jnp.take(middle, accepted, axis=0), upper_rows], axis=1
    )

    slab_width = D // rep_count
    group = rep_count // tp_count
    slabs = local_rows.reshape(rows, 3, group, slab_width)
    mine = jnp.zeros((group, rows, 3, slab_width), jnp.bfloat16)
    for c in range(group):
        perm = []
        for r in range(rep_count):
            for t in range(tp_count):
                s = group * t + (r - c) % group
                perm.append((r * tp_count + t, s * tp_count + r // group))
        block = pick(slabs, (rep_index - c) % group, 2)
        got = lax.ppermute(block, ("rep", "tp"), perm)
        mine = place(mine, got, (rep_index + c) % group)
    mine = mine.reshape(group * rows, 3, slab_width)
    features = place(jnp.zeros((tp_count,) + mine.shape, jnp.bfloat16), mine, tp_index)
    for k, got in enumerate(xor_exchange(lambda k: mine, "tp", tp_count), start=1):
        features = place(features, got, tp_index ^ k)

    total_rows = tp_count * group * rows
    feature_flat = features.reshape(total_rows, 3 * slab_width)
    fc_block = fc_weight.reshape(3 * slab_width, fc_weight.shape[2])
    projected = jnp.dot(feature_flat, fc_block, preferred_element_type=jnp.float32)

    by_chip = projected.reshape(chips, 2, rows, projected.shape[1])
    chip_sum = pick(by_chip, parity, 1) + lax.ppermute(
        pick(by_chip, 1 - parity, 1), "rep", [(i, i ^ 1) for i in range(rep_count)]
    )
    hidden = pick(chip_sum, chip, 0)
    for k in range(1, chips):
        block = pick(chip_sum, chip ^ k, 0).astype(jnp.bfloat16)
        got = lax.ppermute(block, "rep", [(i, i ^ (2 * k)) for i in range(rep_count)])
        hidden = hidden + got.astype(jnp.float32)

    scaled = grad_normed.astype(jnp.float32) * norm_gain
    stats = jnp.stack([jnp.sum(hidden * hidden, axis=1), jnp.sum(scaled * hidden, axis=1)])
    gathered = jnp.stack([stats] + list(xor_exchange(lambda k: stats, "tp", tp_count)))
    stats = jnp.sum(jnp.take(gathered, tp_index ^ jnp.arange(tp_count, dtype=jnp.int32), axis=0), axis=0)
    squares, inner_sum = stats[0], stats[1]
    inv_rms = lax.rsqrt(squares / D + EPSILON)
    normed = (hidden * inv_rms[:, None] * norm_gain).astype(jnp.bfloat16)
    hidden_grads = (
        inv_rms[:, None] * scaled - hidden * (inv_rms**3 * inner_sum / D)[:, None]
    ).astype(jnp.bfloat16)

    same_parity = place(jnp.zeros((chips,) + hidden_grads.shape, jnp.bfloat16), hidden_grads, chip)
    for k in range(1, chips):
        got = lax.ppermute(hidden_grads, "rep", [(i, i ^ (2 * k)) for i in range(rep_count)])
        same_parity = place(same_parity, got, chip ^ k)
    other_parity = lax.ppermute(same_parity, "rep", [(i, i ^ 1) for i in range(rep_count)])
    both = jnp.zeros((2, chips) + hidden_grads.shape, jnp.bfloat16)
    both = place(place(both, same_parity, parity), other_parity, 1 - parity)
    hidden_grads_all = jnp.swapaxes(both, 0, 1).reshape(rep_count * rows, hidden_grads.shape[1])

    grad_fc = lax.dot_general(
        feature_flat, hidden_grads_all, (((0,), (0,)), ((), ())), preferred_element_type=jnp.float32
    )
    grad_fc = grad_fc.reshape(fc_weight.shape).astype(jnp.bfloat16)
    return (normed, grad_fc)


def solution(mesh):
    in_specs = (
        P("rep", "tp"),
        P("rep", "tp"),
        P("rep", "tp"),
        P("rep", "tp"),
        P("rep"),
        P(None, "rep", "tp"),
        P("tp"),
        P("rep", "tp"),
    )
    out_specs = (P("rep", "tp"), P(None, "rep", "tp"))
    return jax.shard_map(body, mesh=mesh, in_specs=in_specs, out_specs=out_specs, check_vma=False)
```

time: 160 us -> 145 us (0.906)
  between operations: 14.4 us -> 0.96 us
  waiting for transfers between devices: 56.2 us -> 47.5 us
  local copies, waits for them, and re-layouts: 20.9 us -> 27.4 us
  starting transfers between devices: 43 us -> 46.8 us
  other arithmetic: 9.95 us -> 8.17 us
    all_gather x1 -> x0, waiting for transfers between devices: 14.8 us -> none  [body(): hidden_grads_all = lax.all_gather(hidden_grads, 'rep', axis=0, tiled=True)]
    dynamic_update_slice x0 -> x11, local copies, waits for them, and re-layouts: none -> 8.84 us  [place(): return lax.dynamic_update_index_in_dim(buffer, piece, index, 0)]
    select_n x2 -> x0, local copies, waits for them, and re-layouts: 8.05 us -> none  [body(): features = jnp.take(jnp.stack(pieces, axis=0), source, axis=0)]
    ppermute x3 -> x7, waiting for transfers between devices: 4.39 us -> 9.63 us  [the longest x3 6.47 us: body(): lax.ppermute(hidden_grads, 'rep', [(i, i ^ 2 * k) for i in range(rep_coun...]
    ppermute x3 -> x7, starting transfers between devices: 0.75 us -> 5.2 us  [the longest x3 4.45 us: body(): lax.ppermute(hidden_grads, 'rep', [(i, i ^ 2 * k) for i in range(rep_coun...]
    gather x4 -> x0, local copies, waits for them, and re-layouts: 4 us -> none  [the longest x2 3.4 us: body(): features = jnp.take(jnp.stack(pieces, axis=0), source, axis=0)]
    dot_general x0 -> x1, local copies, waits for them, and re-layouts: none -> 3.11 us  [body(): jnp.dot(feature_flat, fc_block, preferred_element_type=jnp.float32)]
    ppermute x9, waiting for transfers between devices: 25.3 us -> 27.8 us  [xor_exchange(): yield lax.ppermute(chunk_of(k), axis, perm)]
  transfers between devices with their start and end apart: 16 -> 19, of which waited for: 14 -> 10; matrix products, arithmetic and copies ran while one was open for 5% -> 11% of each run, Pallas kernels for 0% -> 0%
where the time goes in v4:
time: 145 us; the launch traced here: 144 us
  waiting for transfers between devices  47.5 us (33%)
  starting transfers between devices  46.8 us (32%)
  local copies, waits for them, and re-layouts  27.4 us (19%)
  matrix products  13.5 us (9%)
  other arithmetic  8.17 us (6%)
    ppermute x9, starting transfers between devices, xor_exchange(): yield lax.ppermute(chunk_of(k), axis, perm)  38.1 us
    ppermute x9, waiting for transfers between devices, xor_exchange(): yield lax.ppermute(chunk_of(k), axis, perm)  27.8 us
    ppermute x3, waiting for transfers between devices, body(): got = lax.ppermute(block, 'rep', [(i, i ^ 2 * k) for i in range(rep_count)])  10.1 us
    dynamic_update_slice x11, local copies, waits for them, and re-layouts, place(): return lax.dynamic_update_index_in_dim(buffer, piece, index, 0)  8.84 us
    dot_general x1, matrix products, body(): jnp.dot(feature_flat, fc_block, preferred_element_type=jnp.float32)  6.86 us
    dot_general x1, matrix products, body(): lax.dot_general(feature_flat, hidden_grads_all, (((0,), (0,)), ((), ())),...  6.6 us
    ppermute x3, waiting for transfers between devices, body(): lax.ppermute(hidden_grads, 'rep', [(i, i ^ 2 * k) for i in range(rep_coun...  6.47 us
    unnamed x23, local copies, waits for them, and re-layouts  5.55 us
  transfers between devices with their start and end apart: 19, of which 10 were waited for; matrix products, arithmetic and copies ran while one was open for 11% of the time, Pallas kernels for 0%

profile of v4, /device:TPU:0, one launch (start us, length us, event | category | flops | bytes accessed | tf_op | source)
XLA Modules:
  0.0 144.3 jit_solution(2513663393268435526)
XLA Ops:
  0.7 0.7 compare_and_fusion
  1.4 0.7 compare_select_fusion
  2.1 0.9 gather_fusion
  3.0 0.1 bitcast_select_fusion
  3.2 3.0 %collective-permute-start = (bf16[32,2048]{1,0:T(8,128)(2,1)S(1)}, bf16[32,2048]{1,0:T(8,128)(2,1)S(1)}, u32[]{:S(2)}, u32[]{:S(2)}) collective-permute-start(bf16[32,2048]{1,0:T(8,128)(2,1)S(1)} %get-tuple-element.11), channel_id=1, source_target_pairs={{0,1},{1,0},{2,3},{3,2},{4,5},{5,4},{6,7},{7,6},{8,9},{9,8},{10,11... | collective-permute-start | bytes 393224 | tf_op jit(solution)/shard_map/ppermute | solution.py:15
  6.2 1.5 %collective-permute-start.2 = (bf16[32,2048]{1,0:T(8,128)(2,1)S(1)}, bf16[32,2048]{1,0:T(8,128)(2,1)S(1)}, u32[]{:S(2)}, u32[]{:S(2)}) collective-permute-start(bf16[32,2048]{1,0:T(8,128)(2,1)S(1)} %get-tuple-element.12), channel_id=1, source_target_pairs={{0,3},{1,2},{2,1},{3,0},{4,7},{5,6},{6,5},{7,4},{8,11},{9,10},{10,... | collective-permute-start | bytes 393224 | tf_op jit(solution)/shard_map/ppermute | solution.py:15
  7.7 0.6 gather_fusion.4
  8.4 0.7 gather_fusion.3
  9.1 0.7 gather_fusion.2
  9.7 0.1 broadcast_select_fusion
  10.1 3.7 %collective-permute-done.2 = bf16[32,2048]{1,0:T(8,128)(2,1)S(1)} collective-permute-done((bf16[32,2048]{1,0:T(8,128)(2,1)S(1)}, bf16[32,2048]{1,0:T(8,128)(2,1)S(1)}, u32[]{:S(2)}, u32[]{:S(2)}) %collective-permute-start.2) | collective-permute-done | bytes 131104 | tf_op jit(solution)/shard_map/ppermute | solution.py:15
  13.8 1.4 collective-permute-done.1
  15.2 0.1 fusion.3
  15.4 0.7 collective-permute-start.3
  16.2 0.9 broadcast_in_dim.89
  17.2 0.9 copy_dynamic-update-slice_fusion.1
  18.0 0.9 copy_dynamic-update-slice_fusion
  18.9 28.6 %collective-permute-start.5 = (bf16[64,3,1024]{2,1,0:T(4,128)(2,1)}, bf16[64,3,1024]{2,1,0:T(4,128)(2,1)}, u32[]{:S(2)}, u32[]{:S(2)}) collective-permute-start(bf16[64,3,1024]{2,1,0:T(4,128)(2,1)} %bitcast.9), channel_id=1, source_target_pairs={{0,1},{1,0},{2,3},{3,2},{4,5},{5,4},{6,7},{7,6},{8,9},{9,8},{10,11... | collective-permute-start | bytes 1179656 | tf_op jit(solution)/shard_map/ppermute | solution.py:15
  47.5 1.5 %collective-permute-start.7 = (bf16[64,3,1024]{2,1,0:T(4,128)(2,1)}, bf16[64,3,1024]{2,1,0:T(4,128)(2,1)S(1)}, u32[]{:S(2)}, u32[]{:S(2)}) collective-permute-start(bf16[64,3,1024]{2,1,0:T(4,128)(2,1)} %bitcast.9), channel_id=1, source_target_pairs={{0,3},{1,2},{2,1},{3,0},{4,7},{5,6},{6,5},{7,4},{8,11},{9,10},{10,... | collective-permute-start | bytes 1179656 | tf_op jit(solution)/shard_map/ppermute | solution.py:15
  48.9 0.6 broadcast_in_dim.88
  49.6 1.3 bitcast_dynamic-update-slice_fusion.5
  50.8 9.7 %collective-permute-done.5 = bf16[64,3,1024]{2,1,0:T(4,128)(2,1)} collective-permute-done((bf16[64,3,1024]{2,1,0:T(4,128)(2,1)}, bf16[64,3,1024]{2,1,0:T(4,128)(2,1)}, u32[]{:S(2)}, u32[]{:S(2)}) %collective-permute-start.5) | collective-permute-done | bytes 393248 | tf_op jit(solution)/shard_map/ppermute | solution.py:15
  60.5 1.3 bitcast_dynamic-update-slice_fusion.4
  61.8 10.9 %collective-permute-done.6 = bf16[64,3,1024]{2,1,0:T(4,128)(2,1)} collective-permute-done((bf16[64,3,1024]{2,1,0:T(4,128)(2,1)}, bf16[64,3,1024]{2,1,0:T(4,128)(2,1)}, u32[]{:S(2)}, u32[]{:S(2)}) %collective-permute-start.6) | collective-permute-done | bytes 393248 | tf_op jit(solution)/shard_map/ppermute | solution.py:15
  72.7 1.3 bitcast_dynamic-update-slice_fusion.3
  73.9 0.2 bitcast_dynamic-update-slice_fusion.2
  74.2 3.1 %dot_general.12 = bf16[4,2,32,3072]{3,2,1,0:T(8,128)(2,1)} reshape(bf16[4,64,3,1024]{3,2,1,0:T(4,128)(2,1)S(1)} %bitcast_dynamic-update-slice_fusion.2) | data formatting | bytes 3145728 | tf_op jit(solution)/shard_map/dot_general | solution.py:69
  77.3 6.9 %fusion.14 = f32[4,2,32,2048]{3,2,1,0:T(8,128)S(1)} fusion(bf16[4,2,32,3072]{3,2,1,0:T(8,128)(2,1)} %dot_general.12, bf16[3072,2048,1,1]{1,0,3,2:T(8,128)(2,1)} %bitcast.106), kind=kOutput, calls=%fused_computation.66 | convolution fusion | flops 3221225472 | bytes 16252928 | tf_op jit(solution)/shard_map/dot_general | solution.py:69
  84.2 1.3 copy-done.5
  85.5 1.1 dynamic-slice_bitcast_fusion
  86.6 3.0 %collective-permute-done.8 = f32[4,32,2048]{2,1,0:T(8,128)} collective-permute-done((f32[4,32,2048]{2,1,0:T(8,128)}, f32[4,32,2048]{2,1,0:T(8,128)}, u32[]{:S(2)}, u32[]{:S(2)}) %collective-permute-start.8) | collective-permute-done | bytes 1048608 | tf_op jit(solution)/shard_map/ppermute | solution.py:72
  89.6 1.7 %bitcast_add_fusion = f32[4,32,2048]{2,1,0:T(8,128)S(1)} fusion(f32[4,32,2048]{2,1,0:T(8,128)} %collective-permute-done.8, f32[4,2,32,2048]{3,2,1,0:T(8,128)} %copy-done.5, s32[]{:T(128)S(6)} %select_n.122), kind=kLoop, calls=%fused_computation.6 | loop fusion | flops 262144 | bytes 3145732 | tf_op jit(solution)/shard_map/add | solution.py:72
  91.2 1.0 copy-done.4
  92.2 0.7 fusion.6
  92.9 0.6 collective-permute-start.11
  93.5 2.9 %collective-permute-start.10 = (bf16[32,2048]{1,0:T(8,128)(2,1)}, bf16[32,2048]{1,0:T(8,128)(2,1)}, u32[]{:S(2)}, u32[]{:S(2)}) collective-permute-start(bf16[32,2048]{1,0:T(8,128)(2,1)} %get-tuple-element.10), channel_id=1, source_target_pairs={{0,16},{4,20},{8,24},{12,28},{16,0},{20,4},{24,8},{28,12},{1,17},{... | collective-permute-start | bytes 393224 | tf_op jit(solution)/shard_map/ppermute | solution.py:78
  96.4 0.6 pad_clamp_fusion
  97.0 4.5 %collective-permute-done.9 = bf16[32,2048]{1,0:T(8,128)(2,1)S(1)} collective-permute-done((bf16[32,2048]{1,0:T(8,128)(2,1)}, bf16[32,2048]{1,0:T(8,128)(2,1)S(1)}, u32[]{:S(2)}, u32[]{:S(2)}) %collective-permute-start.9) | collective-permute-done | bytes 131104 | tf_op jit(solution)/shard_map/ppermute | solution.py:78
  101.5 0.6 copy-done.7
  102.1 0.7 copy-done.8
  102.8 5.6 %collective-permute-done.10 = bf16[32,2048]{1,0:T(8,128)(2,1)} collective-permute-done((bf16[32,2048]{1,0:T(8,128)(2,1)}, bf16[32,2048]{1,0:T(8,128)(2,1)}, u32[]{:S(2)}, u32[]{:S(2)}) %collective-permute-start.10) | collective-permute-done | bytes 131104 | tf_op jit(solution)/shard_map/ppermute | solution.py:78
  108.4 1.4 multiply_reduce_fusion.1
  109.8 0.4 collective-permute-start.13
  110.2 1.3 collective-permute-start.12
  111.5 1.9 %collective-permute-start.14 = (f32[2,32]{1,0:T(2,128)S(1)}, f32[2,32]{1,0:T(2,128)S(1)}, u32[]{:S(2)}, u32[]{:S(2)}) collective-permute-start(f32[2,32]{1,0:T(2,128)S(1)} %get-tuple-element.17), channel_id=1, source_target_pairs={{0,3},{1,2},{2,1},{3,0},{4,7},{5,6},{6,5},{7,4},{8,11},{9,10},{10,... | collective-permute-start | bytes 776 | tf_op jit(solution)/shard_map/ppermute | solution.py:15
  113.3 0.5 compare_and_fusion.1
  113.9 2.1 %collective-permute-done.14 = f32[2,32]{1,0:T(2,128)S(1)} collective-permute-done((f32[2,32]{1,0:T(2,128)S(1)}, f32[2,32]{1,0:T(2,128)S(1)}, u32[]{:S(2)}, u32[]{:S(2)}) %collective-permute-start.14) | collective-permute-done | bytes 288 | tf_op jit(solution)/shard_map/ppermute | solution.py:15
  116.0 0.7 gather_fusion.1
  116.7 0.7 select_reduce_fusion
  117.4 0.9 broadcast_in_dim.102
  118.3 0.8 bitcast_dynamic-update-slice_fusion.9
  119.1 1.9 %copy.27 = bf16[32,8,3,1024]{3,1,2,0:T(8,128)(2,1)} copy(bf16[32,8,3,1024]{3,2,1,0:T(4,128)(2,1)S(1)} %bitcast.94) | data formatting | bytes 3145728
  121.0 1.7 %copy.24 = bf16[3072,256]{1,0:T(8,128)(2,1)S(1)} copy(bf16[3072,256]{0,1:T(8,128)(2,1)} %bitcast.96) | data formatting | bytes 3145728 | tf_op jit(solution)/shard_map/dot_general | solution.py:101
  122.7 3.3 %collective-permute-start.16 = (bf16[32,2048]{1,0:T(8,128)(2,1)}, bf16[32,2048]{1,0:T(8,128)(2,1)S(1)}, u32[]{:S(2)}, u32[]{:S(2)}) collective-permute-start(bf16[32,2048]{1,0:T(8,128)(2,1)} %get-tuple-element.6), channel_id=1, source_target_pairs={{0,16},{4,20},{8,24},{12,28},{16,0},{20,4},{24,8},{28,12},{1,17},{... | collective-permute-start | bytes 393224 | tf_op jit(solution)/shard_map/ppermute | solution.py:94
  126.0 1.2 collective-permute-start.17
  127.1 0.6 bitcast_dynamic-update-slice_fusion.8
  127.8 6.5 %collective-permute-done.16 = bf16[32,2048]{1,0:T(8,128)(2,1)S(1)} collective-permute-done((bf16[32,2048]{1,0:T(8,128)(2,1)}, bf16[32,2048]{1,0:T(8,128)(2,1)S(1)}, u32[]{:S(2)}, u32[]{:S(2)}) %collective-permute-start.16) | collective-permute-done | bytes 131104 | tf_op jit(solution)/shard_map/ppermute | solution.py:94
  134.3 0.7 bitcast_dynamic-update-slice_fusion.7
  134.9 0.7 bitcast_dynamic-update-slice_fusion.6
  135.6 0.7 multiply_convert_fusion
  136.3 0.1 broadcast_in_dim.101
  136.4 1.1 bitcast_dynamic-update-slice_fusion.1
  137.5 0.2 collective-permute-done.18
  137.7 6.6 %convolution_convert_fusion = bf16[3,1024,2048]{2,1,0:T(8,128)(2,1)} fusion(bf16[3,1024,256]{2,1,0:T(8,128)(2,1)S(1)} %bitcast.95, bf16[256,2048,1]{1,0,2:T(8,128)(2,1)S(1)} %bitcast.97), kind=kOutput, calls=%fused_computation.5 | convolution fusion | flops 3227516928 | bytes 15204352 | tf_op jit(solution)/shard_map/dot_general | solution.py:101
  (47 shorter events, 0.7 us)
Async XLA Ops:
  0.6 1.4 %copy-start = (bf16[64,8192]{1,0:T(8,128)(2,1)S(1)}, bf16[64,8192]{1,0:T(8,128)(2,1)}, u32[]{:S(2)}) copy-start(bf16[64,8192]{1,0:T(8,128)(2,1)} %param.10) | copy-start | bytes 3145732
  3.0 4.8 %copy-start.1 = (bf16[64,2048]{1,0:T(8,128)(2,1)S(1)}, bf16[64,2048]{1,0:T(8,128)(2,1)}, u32[]{:S(2)}) copy-start(bf16[64,2048]{1,0:T(8,128)(2,1)} %param.11) | copy-start | bytes 786436
  3.0 5.4 %copy-start.2 = (bf16[64,2048]{1,0:T(8,128)(2,1)S(1)}, bf16[64,2048]{1,0:T(8,128)(2,1)}, u32[]{:S(2)}) copy-start(bf16[64,2048]{1,0:T(8,128)(2,1)} %param.13) | copy-start | bytes 786436
  3.0 6.1 %copy-start.3 = (bf16[64,2048]{1,0:T(8,128)(2,1)S(1)}, bf16[64,2048]{1,0:T(8,128)(2,1)}, u32[]{:S(2)}) copy-start(bf16[64,2048]{1,0:T(8,128)(2,1)} %param.12) | copy-start | bytes 786436
  3.2 6.9 %collective-permute-start = (bf16[32,2048]{1,0:T(8,128)(2,1)S(1)}, bf16[32,2048]{1,0:T(8,128)(2,1)S(1)}, u32[]{:S(2)}, u32[]{:S(2)}) collective-permute-start(bf16[32,2048]{1,0:T(8,128)(2,1)S(1)} %get-tuple-element.11), channel_id=1, source_target_pairs={{0,1},{1,0},{2,3},{3,2},{4,5},{5,4},{6,7},{7,6},{8,9},{9,8},{10,11... | collective-permute-start | bytes 393224 | tf_op jit(solution)/shard_map/ppermute | solution.py:15
  6.2 7.6 %collective-permute-start.2 = (bf16[32,2048]{1,0:T(8,128)(2,1)S(1)}, bf16[32,2048]{1,0:T(8,128)(2,1)S(1)}, u32[]{:S(2)}, u32[]{:S(2)}) collective-permute-start(bf16[32,2048]{1,0:T(8,128)(2,1)S(1)} %get-tuple-element.12), channel_id=1, source_target_pairs={{0,3},{1,2},{2,1},{3,0},{4,7},{5,6},{6,5},{7,4},{8,11},{9,10},{10,... | collective-permute-start | bytes 393224 | tf_op jit(solution)/shard_map/ppermute | solution.py:15
  7.7 7.5 %collective-permute-start.1 = (bf16[32,2048]{1,0:T(8,128)(2,1)S(1)}, bf16[32,2048]{1,0:T(8,128)(2,1)S(1)}, u32[]{:S(2)}, u32[]{:S(2)}) collective-permute-start(bf16[32,2048]{1,0:T(8,128)(2,1)S(1)} %get-tuple-element.13), channel_id=1, source_target_pairs={{0,2},{1,3},{2,0},{3,1},{4,6},{5,7},{6,4},{7,5},{8,10},{9,11},{10,... | collective-permute-start | bytes 393224 | tf_op jit(solution)/shard_map/ppermute | solution.py:15
  15.4 0.8 collective-permute-start.3
  16.1 1.9 %collective-permute-start.4 = (bf16[32,3,1024]{2,0,1:T(8,128)(2,1)S(1)}, bf16[32,3,1024]{2,0,1:T(8,128)(2,1)S(1)}, u32[]{:S(2)}, u32[]{:S(2)}) collective-permute-start(bf16[32,3,1024]{2,0,1:T(8,128)(2,1)S(1)} %get-tuple-element.14), channel_id=1, source_target_pairs={{0,4},{1,12},{2,20},{3,28},{4,0},{5,8},{6,16},{7,24},{8,5},{9,13},... | collective-permute-start | bytes 589832 | tf_op jit(solution)/shard_map/ppermute | solution.py:59
  18.9 41.6 %collective-permute-start.5 = (bf16[64,3,1024]{2,1,0:T(4,128)(2,1)}, bf16[64,3,1024]{2,1,0:T(4,128)(2,1)}, u32[]{:S(2)}, u32[]{:S(2)}) collective-permute-start(bf16[64,3,1024]{2,1,0:T(4,128)(2,1)} %bitcast.9), channel_id=1, source_target_pairs={{0,1},{1,0},{2,3},{3,2},{4,5},{5,4},{6,7},{7,6},{8,9},{9,8},{10,11... | collective-permute-start | bytes 1179656 | tf_op jit(solution)/shard_map/ppermute | solution.py:15
  47.5 25.2 %collective-permute-start.6 = (bf16[64,3,1024]{2,1,0:T(4,128)(2,1)}, bf16[64,3,1024]{2,1,0:T(4,128)(2,1)}, u32[]{:S(2)}, u32[]{:S(2)}) collective-permute-start(bf16[64,3,1024]{2,1,0:T(4,128)(2,1)} %bitcast.9), channel_id=1, source_target_pairs={{0,2},{1,3},{2,0},{3,1},{4,6},{5,7},{6,4},{7,5},{8,10},{9,11},{10,... | collective-permute-start | bytes 1179656 | tf_op jit(solution)/shard_map/ppermute | solution.py:15
  47.5 26.5 %collective-permute-start.7 = (bf16[64,3,1024]{2,1,0:T(4,128)(2,1)}, bf16[64,3,1024]{2,1,0:T(4,128)(2,1)S(1)}, u32[]{:S(2)}, u32[]{:S(2)}) collective-permute-start(bf16[64,3,1024]{2,1,0:T(4,128)(2,1)} %bitcast.9), channel_id=1, source_target_pairs={{0,3},{1,2},{2,1},{3,0},{4,7},{5,6},{6,5},{7,4},{8,11},{9,10},{10,... | collective-permute-start | bytes 1179656 | tf_op jit(solution)/shard_map/ppermute | solution.py:15
  84.2 1.3 copy-start.5
  86.6 21.8 %copy-start.6 = (bf16[32,2048]{1,0:T(8,128)(2,1)S(1)}, bf16[32,2048]{1,0:T(8,128)(2,1)}, u32[]{:S(2)}) copy-start(bf16[32,2048]{1,0:T(8,128)(2,1)} %param.17) | copy-start | bytes 393220
  86.6 21.8 %copy-start.9 = (f32[2048]{0:T(1024)S(1)}, f32[2048]{0:T(1024)}, u32[]{:S(2)}) copy-start(f32[2048]{0:T(1024)} %param.16) | copy-start | bytes 24580
  86.6 3.0 %collective-permute-start.8 = (f32[4,32,2048]{2,1,0:T(8,128)}, f32[4,32,2048]{2,1,0:T(8,128)}, u32[]{:S(2)}, u32[]{:S(2)}) collective-permute-start(f32[4,32,2048]{2,1,0:T(8,128)} %dynamic-slice_bitcast_fusion), channel_id=1, source_target_pairs={{0,4},{4,0},{8,12},{12,8},{16,20},{20,16},{24,28},{28,24},{1,5},{5... | collective-permute-start | bytes 3145736 | tf_op jit(solution)/shard_map/ppermute | solution.py:72
  91.2 1.0 copy-start.4
  92.9 8.6 %collective-permute-start.9 = (bf16[32,2048]{1,0:T(8,128)(2,1)}, bf16[32,2048]{1,0:T(8,128)(2,1)S(1)}, u32[]{:S(2)}, u32[]{:S(2)}) collective-permute-start(bf16[32,2048]{1,0:T(8,128)(2,1)} %get-tuple-element.8), channel_id=1, source_target_pairs={{0,8},{4,12},{8,0},{12,4},{16,24},{20,28},{24,16},{28,20},{1,9},{5... | collective-permute-start | bytes 393224 | tf_op jit(solution)/shard_map/ppermute | solution.py:78
  92.9 8.6 %collective-permute-start.11 = (bf16[32,2048]{1,0:T(8,128)(2,1)}, bf16[32,2048]{1,0:T(8,128)(2,1)S(1)}, u32[]{:S(2)}, u32[]{:S(2)}) collective-permute-start(bf16[32,2048]{1,0:T(8,128)(2,1)} %get-tuple-element.9), channel_id=1, source_target_pairs={{0,24},{4,28},{8,16},{12,20},{16,8},{20,12},{24,0},{28,4},{1,25},{... | collective-permute-start | bytes 393224 | tf_op jit(solution)/shard_map/ppermute | solution.py:78
  93.5 14.9 %collective-permute-start.10 = (bf16[32,2048]{1,0:T(8,128)(2,1)}, bf16[32,2048]{1,0:T(8,128)(2,1)}, u32[]{:S(2)}, u32[]{:S(2)}) collective-permute-start(bf16[32,2048]{1,0:T(8,128)(2,1)} %get-tuple-element.10), channel_id=1, source_target_pairs={{0,16},{4,20},{8,24},{12,28},{16,0},{20,4},{24,8},{28,12},{1,17},{... | collective-permute-start | bytes 393224 | tf_op jit(solution)/shard_map/ppermute | solution.py:78
  101.5 0.6 copy-start.7
  102.1 0.7 copy-start.8
  109.8 4.1 %collective-permute-start.13 = (f32[2,32]{1,0:T(2,128)S(1)}, f32[2,32]{1,0:T(2,128)S(1)}, u32[]{:S(2)}, u32[]{:S(2)}) collective-permute-start(f32[2,32]{1,0:T(2,128)S(1)} %get-tuple-element.17), channel_id=1, source_target_pairs={{0,2},{1,3},{2,0},{3,1},{4,6},{5,7},{6,4},{7,5},{8,10},{9,11},{10,... | collective-permute-start | bytes 776 | tf_op jit(solution)/shard_map/ppermute | solution.py:15
  110.2 3.7 %collective-permute-start.12 = (f32[2,32]{1,0:T(2,128)S(1)}, f32[2,32]{1,0:T(2,128)S(1)}, u32[]{:S(2)}, u32[]{:S(2)}) collective-permute-start(f32[2,32]{1,0:T(2,128)S(1)} %get-tuple-element.17), channel_id=1, source_target_pairs={{0,1},{1,0},{2,3},{3,2},{4,5},{5,4},{6,7},{7,6},{8,9},{9,8},{10,11... | collective-permute-start | bytes 776 | tf_op jit(solution)/shard_map/ppermute | solution.py:15
  111.5 4.5 %collective-permute-start.14 = (f32[2,32]{1,0:T(2,128)S(1)}, f32[2,32]{1,0:T(2,128)S(1)}, u32[]{:S(2)}, u32[]{:S(2)}) collective-permute-start(f32[2,32]{1,0:T(2,128)S(1)} %get-tuple-element.17), channel_id=1, source_target_pairs={{0,3},{1,2},{2,1},{3,0},{4,7},{5,6},{6,5},{7,4},{8,11},{9,10},{10,... | collective-permute-start | bytes 776 | tf_op jit(solution)/shard_map/ppermute | solution.py:15
  119.1 8.1 %collective-permute-start.15 = (bf16[32,2048]{1,0:T(8,128)(2,1)}, bf16[32,2048]{1,0:T(8,128)(2,1)S(1)}, u32[]{:S(2)}, u32[]{:S(2)}) collective-permute-start(bf16[32,2048]{1,0:T(8,128)(2,1)} %get-tuple-element.6), channel_id=1, source_target_pairs={{0,8},{4,12},{8,0},{12,4},{16,24},{20,28},{24,16},{28,20},{1,9},{5... | collective-permute-start | bytes 393224 | tf_op jit(solution)/shard_map/ppermute | solution.py:94
  122.7 11.6 %collective-permute-start.16 = (bf16[32,2048]{1,0:T(8,128)(2,1)}, bf16[32,2048]{1,0:T(8,128)(2,1)S(1)}, u32[]{:S(2)}, u32[]{:S(2)}) collective-permute-start(bf16[32,2048]{1,0:T(8,128)(2,1)} %get-tuple-element.6), channel_id=1, source_target_pairs={{0,16},{4,20},{8,24},{12,28},{16,0},{20,4},{24,8},{28,12},{1,17},{... | collective-permute-start | bytes 393224 | tf_op jit(solution)/shard_map/ppermute | solution.py:94
  126.0 9.0 %collective-permute-start.17 = (bf16[32,2048]{1,0:T(8,128)(2,1)}, bf16[32,2048]{1,0:T(8,128)(2,1)S(1)}, u32[]{:S(2)}, u32[]{:S(2)}) collective-permute-start(bf16[32,2048]{1,0:T(8,128)(2,1)} %get-tuple-element.6), channel_id=1, source_target_pairs={{0,24},{4,28},{8,16},{12,20},{16,8},{20,12},{24,0},{28,4},{1,25},{... | collective-permute-start | bytes 393224 | tf_op jit(solution)/shard_map/ppermute | solution.py:94
  135.6 2.1 %collective-permute-start.18 = (bf16[4,32,2048]{2,1,0:T(8,128)(2,1)}, bf16[4,32,2048]{2,1,0:T(8,128)(2,1)S(1)}, u32[]{:S(2)}, u32[]{:S(2)}) collective-permute-start(bf16[4,32,2048]{2,1,0:T(8,128)(2,1)} %bitcast_dynamic-update-slice_fusion.6), channel_id=1, source_target_pairs={{0,4},{4,0},{8,12},{12,8},{16,20},{20,16},{24,28},{28,24},{1,5},{5... | collective-permute-start | bytes 1572872 | tf_op jit(solution)/shard_map/ppermute | solution.py:96

commit v5 on v4

--- a/solution.py
+++ b/solution.py
@@ -41,32 +41,36 @@
     upper_rows = (jnp.take(residual, accepted, axis=0).astype(jnp.float32) + summed).astype(
         jnp.bfloat16
     )
-    local_rows = jnp.stack(
-        [jnp.take(lower, accepted, axis=0), jnp.take(middle, accepted, axis=0), upper_rows], axis=1
-    )
 
     slab_width = D // rep_count
     group = rep_count // tp_count
-    slabs = local_rows.reshape(rows, 3, group, slab_width)
-    mine = jnp.zeros((group, rows, 3, slab_width), jnp.bfloat16)
-    for c in range(group):
-        perm = []
-        for r in range(rep_count):
-            for t in range(tp_count):
-                s = group * t + (r - c) % group
-                perm.append((r * tp_count + t, s * tp_count + r // group))
-        block = pick(slabs, (rep_index - c) % group, 2)
-        got = lax.ppermute(block, ("rep", "tp"), perm)
-        mine = place(mine, got, (rep_index + c) % group)
-    mine = mine.reshape(group * rows, 3, slab_width)
-    features = place(jnp.zeros((tp_count,) + mine.shape, jnp.bfloat16), mine, tp_index)
-    for k, got in enumerate(xor_exchange(lambda k: mine, "tp", tp_count), start=1):
-        features = place(features, got, tp_index ^ k)
 
-    total_rows = tp_count * group * rows
-    feature_flat = features.reshape(total_rows, 3 * slab_width)
-    fc_block = fc_weight.reshape(3 * slab_width, fc_weight.shape[2])
-    projected = jnp.dot(feature_flat, fc_block, preferred_element_type=jnp.float32)
+    def relayout(kind_rows):
+        slabs = kind_rows.reshape(rows, group, slab_width)
+        mine = jnp.zeros((group, rows, slab_width), jnp.bfloat16)
+        for c in range(group):
+            perm = []
+            for r in range(rep_count):
+                for t in range(tp_count):
+                    s = group * t + (r - c) % group
+                    perm.append((r * tp_count + t, s * tp_count + r // group))
+            block = pick(slabs, (rep_index - c) % group, 1)
+            got = lax.ppermute(block, ("rep", "tp"), perm)
+            mine = place(mine, got, (rep_index + c) % group)
+        mine = mine.reshape(group * rows, slab_width)
+        gathered = place(jnp.zeros((tp_count,) + mine.shape, jnp.bfloat16), mine, tp_index)
+        for k, got in enumerate(xor_exchange(lambda k: mine, "tp", tp_count), start=1):
+            gathered = place(gathered, got, tp_index ^ k)
+        return gathered.reshape(tp_count * group * rows, slab_width)
+
+    kinds = [
+        relayout(jnp.take(lower, accepted, axis=0)),
+        relayout(jnp.take(middle, accepted, axis=0)),
+        relayout(upper_rows),
+    ]
+    projected = jnp.dot(kinds[0], fc_weight[0], preferred_element_type=jnp.float32)
+    for l in (1, 2):
+        projected = projected + jnp.dot(kinds[l], fc_weight[l], preferred_element_type=jnp.float32)
 
     by_chip = projected.reshape(chips, 2, rows, projected.shape[1])
     chip_sum = pick(by_chip, parity, 1) + lax.ppermute(
@@ -98,10 +102,14 @@
     both = place(place(both, same_parity, parity), other_parity, 1 - parity)
     hidden_grads_all = jnp.swapaxes(both, 0, 1).reshape(rep_count * rows, hidden_grads.shape[1])
 
-    grad_fc = lax.dot_general(
-        feature_flat, hidden_grads_all, (((0,), (0,)), ((), ())), preferred_element_type=jnp.float32
+    grad_fc = jnp.stack(
+        [
+            lax.dot_general(
+                kind, hidden_grads_all, (((0,), (0,)), ((), ())), preferred_element_type=jnp.float32
+            ).astype(jnp.bfloat16)
+            for kind in kinds
+        ]
     )
-    grad_fc = grad_fc.reshape(fc_weight.shape).astype(jnp.bfloat16)
     return (normed, grad_fc)
 
 

time: 145 us -> 131 us (0.903)
  local copies, waits for them, and re-layouts: 27.4 us -> 9.72 us
  starting transfers between devices: 46.8 us -> 60.2 us
  waiting for transfers between devices: 47.5 us -> 34.3 us
  other arithmetic: 8.17 us -> 10.6 us
    ppermute x9 -> x15, waiting for transfers between devices: 27.8 us -> 11.1 us  [xor_exchange(): yield lax.ppermute(chunk_of(k), axis, perm)]
    ppermute x9 -> x15, starting transfers between devices: 38.1 us -> 48.9 us  [xor_exchange(): yield lax.ppermute(chunk_of(k), axis, perm)]
    dynamic_update_slice x11 -> x23, local copies, waits for them, and re-layouts: 8.84 us -> 0.4 us  [place(): return lax.dynamic_update_index_in_dim(buffer, piece, index, 0)]
    another operation x0 -> x1, other arithmetic: none -> 5.38 us  [body(): jnp.stack([lax.dot_general(kind, hidden_grads_all, (((0,), (0,)), ((), ()...]
    dot_general x2 -> x0, local copies, waits for them, and re-layouts: 4.81 us -> none  [the longest x1 3.11 us: body(): jnp.dot(feature_flat, fc_block, preferred_element_type=jnp.float32)]
    unnamed x23 -> x28, local copies, waits for them, and re-layouts: 5.55 us -> 1.18 us
    ppermute x2 -> x6, starting transfers between devices: 0.74 us -> 3.28 us  [relayout(): got = lax.ppermute(block, ('rep', 'tp'), perm)]
    ppermute x3, waiting for transfers between devices: 10.1 us -> 11.6 us  [body(): got = lax.ppermute(block, 'rep', [(i, i ^ 2 * k) for i in range(rep_count)])]
  transfers between devices with their start and end apart: 19 -> 29, of which waited for: 10 -> 14; matrix products, arithmetic and copies ran while one was open for 11% -> 6% of each run, Pallas kernels for 0% -> 0%
where the time goes in v5:
time: 131 us
  starting transfers between devices  60.2 us (46%)
  waiting for transfers between devices  34.3 us (26%)
  matrix products  14.7 us (11%)
  other arithmetic  10.6 us (8%)
  local copies, waits for them, and re-layouts  9.72 us (7%)
  between operations  1.39 us (1%)
    ppermute x15, starting transfers between devices, xor_exchange(): yield lax.ppermute(chunk_of(k), axis, perm)  48.9 us
    ppermute x3, waiting for transfers between devices, body(): got = lax.ppermute(block, 'rep', [(i, i ^ 2 * k) for i in range(rep_count)])  11.6 us
    ppermute x15, waiting for transfers between devices, xor_exchange(): yield lax.ppermute(chunk_of(k), axis, perm)  11.1 us
    dot_general x2, matrix products, body(): jnp.dot(kinds[l], fc_weight[l], preferred_element_type=jnp.float32)  7.27 us
    ppermute x3, waiting for transfers between devices, body(): lax.ppermute(hidden_grads, 'rep', [(i, i ^ 2 * k) for i in range(rep_coun...  6.66 us
    another operation x1, other arithmetic, body(): jnp.stack([lax.dot_general(kind, hidden_grads_all, (((0,), (0,)), ((), ()...  5.38 us
    ppermute x3, starting transfers between devices, body(): lax.ppermute(hidden_grads, 'rep', [(i, i ^ 2 * k) for i in range(rep_coun...  4.44 us
    dot_general x3, matrix products, body(): lax.dot_general(kind, hidden_grads_all, (((0,), (0,)), ((), ())), preferr...  3.87 us
  transfers between devices with their start and end apart: 29, of which 14 were waited for; matrix products, arithmetic and copies ran while one was open for 6% of the time, Pallas kernels for 0%

profile of v5, /device:TPU:0, one launch (start us, length us, event | category | flops | bytes accessed | tf_op | source)
XLA Modules:
  0.0 130.9 jit_solution(6867332784279091725)
XLA Ops:
  0.7 0.7 compare_and_fusion
  1.4 0.7 compare_select_fusion
  2.1 1.7 %gather_fusion.3 = bf16[32,2048]{1,0:T(8,128)(2,1)S(1)} fusion(bf16[64,2048]{1,0:T(8,128)(2,1)} %param.13, s32[1024]{0:T(1024)S(1)} %pad_clamp_fusion.1), kind=kCustom, calls=%fused_computation.1.clone | custom fusion | bytes 262272 | tf_op jit(solution)/shard_map/jit(_take)/gather | solution.py:68
  3.8 1.8 %gather_fusion.2 = bf16[32,2048]{1,0:T(8,128)(2,1)S(1)} fusion(bf16[64,2048]{1,0:T(8,128)(2,1)} %param.12, s32[1024]{0:T(1024)S(1)} %pad_clamp_fusion.1), kind=kCustom, calls=%fused_computation.clone | custom fusion | bytes 262272 | tf_op jit(solution)/shard_map/jit(_take)/gather | solution.py:67
  5.6 0.1 broadcast_select_fusion.1
  5.7 0.1 reshape.107
  5.8 0.3 constant_dynamic-slice_fusion.4
  6.1 0.7 collective-permute-start
  6.8 0.6 collective-permute-start.1
  7.4 0.9 gather_fusion
  8.3 0.1 bitcast_select_fusion
  8.5 5.9 %collective-permute-start.10 = (bf16[32,2048]{1,0:T(8,128)(2,1)S(1)}, bf16[32,2048]{1,0:T(8,128)(2,1)S(1)}, u32[]{:S(2)}, u32[]{:S(2)}) collective-permute-start(bf16[32,2048]{1,0:T(8,128)(2,1)S(1)} %get-tuple-element.11), channel_id=1, source_target_pairs={{0,1},{1,0},{2,3},{3,2},{4,5},{5,4},{6,7},{7,6},{8,9},{9,8},{10,11... | collective-permute-start | bytes 393224 | tf_op jit(solution)/shard_map/ppermute | solution.py:15
  14.3 3.7 %collective-permute-start.12 = (bf16[32,2048]{1,0:T(8,128)(2,1)S(1)}, bf16[32,2048]{1,0:T(8,128)(2,1)S(1)}, u32[]{:S(2)}, u32[]{:S(2)}) collective-permute-start(bf16[32,2048]{1,0:T(8,128)(2,1)S(1)} %get-tuple-element.12), channel_id=1, source_target_pairs={{0,3},{1,2},{2,1},{3,0},{4,7},{5,6},{6,5},{7,4},{8,11},{9,10},{10,... | collective-permute-start | bytes 393224 | tf_op jit(solution)/shard_map/ppermute | solution.py:15
  18.1 0.5 collective-permute-start.11
  18.5 0.6 gather_fusion.4
  19.4 4.3 %collective-permute-start.4 = (bf16[64,1024]{1,0:T(8,128)(2,1)S(1)}, bf16[64,1024]{1,0:T(8,128)(2,1)S(1)}, u32[]{:S(2)}, u32[]{:S(2)}) collective-permute-start(bf16[64,1024]{1,0:T(8,128)(2,1)S(1)} %bitcast.167), channel_id=1, source_target_pairs={{0,3},{1,2},{2,1},{3,0},{4,7},{5,6},{6,5},{7,4},{8,11},{9,10},{10,... | collective-permute-start | bytes 393224 | tf_op jit(solution)/shard_map/ppermute | solution.py:15
  23.7 0.7 collective-permute-start.3
  24.4 0.6 collective-permute-done.12
  25.0 5.1 %collective-permute-done.11 = bf16[32,2048]{1,0:T(8,128)(2,1)S(1)} collective-permute-done((bf16[32,2048]{1,0:T(8,128)(2,1)S(1)}, bf16[32,2048]{1,0:T(8,128)(2,1)S(1)}, u32[]{:S(2)}, u32[]{:S(2)}) %collective-permute-start.11) | collective-permute-done | bytes 131104 | tf_op jit(solution)/shard_map/ppermute | solution.py:15
  30.0 0.1 fusion.18
  30.2 0.5 constant_dynamic-slice_fusion
  30.8 0.7 collective-permute-start.13
  31.8 0.5 collective-permute-start.14
  32.3 0.9 collective-permute-done.14
  33.2 0.8 collective-permute-start.5
  34.0 20.7 %collective-permute-start.17 = (bf16[64,1024]{1,0:T(8,128)(2,1)S(1)}, bf16[64,1024]{1,0:T(8,128)(2,1)S(1)}, u32[]{:S(2)}, u32[]{:S(2)}) collective-permute-start(bf16[64,1024]{1,0:T(8,128)(2,1)S(1)} %bitcast.171), channel_id=1, source_target_pairs={{0,3},{1,2},{2,1},{3,0},{4,7},{5,6},{6,5},{7,4},{8,11},{9,10},{10,... | collective-permute-start | bytes 393224 | tf_op jit(solution)/shard_map/ppermute | solution.py:15
  54.8 0.6 collective-permute-start.16
  55.4 5.1 %collective-permute-start.15 = (bf16[64,1024]{1,0:T(8,128)(2,1)S(1)}, bf16[64,1024]{1,0:T(8,128)(2,1)S(1)}, u32[]{:S(2)}, u32[]{:S(2)}) collective-permute-start(bf16[64,1024]{1,0:T(8,128)(2,1)S(1)} %bitcast.173), channel_id=1, source_target_pairs={{0,1},{1,0},{2,3},{3,2},{4,5},{5,4},{6,7},{7,6},{8,9},{9,8},{10,11... | collective-permute-start | bytes 393224 | tf_op jit(solution)/shard_map/ppermute | solution.py:15
  60.5 0.6 collective-permute-start.9
  61.1 1.0 collective-permute-start.8
  62.3 1.6 %collective-permute-done.15 = bf16[64,1024]{1,0:T(8,128)(2,1)S(1)} collective-permute-done((bf16[64,1024]{1,0:T(8,128)(2,1)S(1)}, bf16[64,1024]{1,0:T(8,128)(2,1)S(1)}, u32[]{:S(2)}, u32[]{:S(2)}) %collective-permute-start.15) | collective-permute-done | bytes 131104 | tf_op jit(solution)/shard_map/ppermute | solution.py:15
  63.9 2.3 %collective-permute-start.7 = (bf16[64,1024]{1,0:T(8,128)(2,1)S(1)}, bf16[64,1024]{1,0:T(8,128)(2,1)S(1)}, u32[]{:S(2)}, u32[]{:S(2)}) collective-permute-start(bf16[64,1024]{1,0:T(8,128)(2,1)S(1)} %bitcast.178), channel_id=1, source_target_pairs={{0,1},{1,0},{2,3},{3,2},{4,5},{5,4},{6,7},{7,6},{8,9},{9,8},{10,11... | collective-permute-start | bytes 393224 | tf_op jit(solution)/shard_map/ppermute | solution.py:15
  66.3 3.6 %fusion = f32[256,2048]{1,0:T(8,128)S(1)} fusion(bf16[256,1024]{1,0:T(8,128)(2,1)S(1)} %bitcast.162, bf16[3,1024,2048]{2,1,0:T(8,128)(2,1)} %param.15), kind=kOutput, calls=%fused_computation.6 | convolution fusion | flops 1073741824 | bytes 6815744 | tf_op jit(solution)/shard_map/dot_general | solution.py:73
  70.1 3.6 %fusion.2 = f32[256,2048]{1,0:T(8,128)S(1)} fusion(bf16[256,1024]{1,0:T(8,128)(2,1)S(1)} %bitcast.164, bf16[3,1024,2048]{2,1,0:T(8,128)(2,1)} %param.15), kind=kOutput, calls=%fused_computation.8 | convolution fusion | flops 1073741824 | bytes 6815744 | tf_op jit(solution)/shard_map/dot_general | solution.py:73
  73.7 3.6 %fusion.12 = f32[256,2048]{1,0:T(8,128)S(1)} fusion(f32[256,2048]{1,0:T(8,128)S(1)} %fusion, f32[256,2048]{1,0:T(8,128)S(1)} %fusion.2, bf16[256,1024]{1,0:T(8,128)(2,1)S(1)} %bitcast.160, bf16[3,1024,2048]{2,1,0:T(8,128)(2,1)} %param.15), kind=kOutput, calls=%fused_computation.19 | convolution fusion | flops 1074790400 | bytes 11010048 | tf_op jit(solution)/shard_map/dot_general | solution.py:71
  77.4 1.0 dynamic-slice_bitcast_fusion
  78.4 3.0 %collective-permute-done.18 = f32[4,32,2048]{2,1,0:T(8,128)} collective-permute-done((f32[4,32,2048]{2,1,0:T(8,128)}, f32[4,32,2048]{2,1,0:T(8,128)}, u32[]{:S(2)}, u32[]{:S(2)}) %collective-permute-start.18) | collective-permute-done | bytes 1048608 | tf_op jit(solution)/shard_map/ppermute | solution.py:76
  81.4 1.3 %bitcast_add_fusion = f32[4,32,2048]{2,1,0:T(8,128)S(1)} fusion(f32[4,32,2048]{2,1,0:T(8,128)} %collective-permute-done.18, f32[4,2,32,2048]{3,2,1,0:T(8,128)S(1)} %bitcast.159, s32[]{:T(128)S(6)} %select_n.148), kind=kLoop, calls=%fused_computation.20 | loop fusion | flops 262144 | bytes 3145732 | tf_op jit(solution)/shard_map/add | solution.py:76
  82.8 1.0 copy-done.8
  83.9 2.7 %collective-permute-start.21 = (bf16[32,2048]{1,0:T(8,128)(2,1)S(1)}, bf16[32,2048]{1,0:T(8,128)(2,1)S(1)}, u32[]{:S(2)}, u32[]{:S(2)}) collective-permute-start(bf16[32,2048]{1,0:T(8,128)(2,1)S(1)} %get-tuple-element.9), channel_id=1, source_target_pairs={{0,24},{4,28},{8,16},{12,20},{16,8},{20,12},{24,0},{28,4},{1,25},{... | collective-permute-start | bytes 393224 | tf_op jit(solution)/shard_map/ppermute | solution.py:82
  86.6 0.8 collective-permute-start.20
  87.3 2.0 %collective-permute-done.19 = bf16[32,2048]{1,0:T(8,128)(2,1)S(1)} collective-permute-done((bf16[32,2048]{1,0:T(8,128)(2,1)S(1)}, bf16[32,2048]{1,0:T(8,128)(2,1)S(1)}, u32[]{:S(2)}, u32[]{:S(2)}) %collective-permute-start.19) | collective-permute-done | bytes 131104 | tf_op jit(solution)/shard_map/ppermute | solution.py:82
  89.4 4.4 %collective-permute-done.21 = bf16[32,2048]{1,0:T(8,128)(2,1)S(1)} collective-permute-done((bf16[32,2048]{1,0:T(8,128)(2,1)S(1)}, bf16[32,2048]{1,0:T(8,128)(2,1)S(1)}, u32[]{:S(2)}, u32[]{:S(2)}) %collective-permute-start.21) | collective-permute-done | bytes 131104 | tf_op jit(solution)/shard_map/ppermute | solution.py:82
  93.7 5.2 %collective-permute-done.20 = bf16[32,2048]{1,0:T(8,128)(2,1)S(1)} collective-permute-done((bf16[32,2048]{1,0:T(8,128)(2,1)S(1)}, bf16[32,2048]{1,0:T(8,128)(2,1)S(1)}, u32[]{:S(2)}, u32[]{:S(2)}) %collective-permute-start.20) | collective-permute-done | bytes 131104 | tf_op jit(solution)/shard_map/ppermute | solution.py:82
  99.0 1.2 multiply_reduce_fusion.1
  100.2 1.7 %collective-permute-start.23 = (f32[2,32]{1,0:T(2,128)S(1)}, f32[2,32]{1,0:T(2,128)S(1)}, u32[]{:S(2)}, u32[]{:S(2)}) collective-permute-start(f32[2,32]{1,0:T(2,128)S(1)} %get-tuple-element.21), channel_id=1, source_target_pairs={{0,2},{1,3},{2,0},{3,1},{4,6},{5,7},{6,4},{7,5},{8,10},{9,11},{10,... | collective-permute-start | bytes 776 | tf_op jit(solution)/shard_map/ppermute | solution.py:15
  101.9 1.2 collective-permute-start.22
  103.1 0.6 collective-permute-start.24
  103.8 1.6 %collective-permute-done.22 = f32[2,32]{1,0:T(2,128)S(1)} collective-permute-done((f32[2,32]{1,0:T(2,128)S(1)}, f32[2,32]{1,0:T(2,128)S(1)}, u32[]{:S(2)}, u32[]{:S(2)}) %collective-permute-start.22) | collective-permute-done | bytes 288 | tf_op jit(solution)/shard_map/ppermute | solution.py:15
  105.4 2.1 %collective-permute-done.24 = f32[2,32]{1,0:T(2,128)S(1)} collective-permute-done((f32[2,32]{1,0:T(2,128)S(1)}, f32[2,32]{1,0:T(2,128)S(1)}, u32[]{:S(2)}, u32[]{:S(2)}) %collective-permute-start.24) | collective-permute-done | bytes 288 | tf_op jit(solution)/shard_map/ppermute | solution.py:15
  107.6 0.6 gather_fusion.1
  108.1 0.1 select_reduce_fusion
  108.3 0.1 bitcast_dynamic-update-slice_fusion.5
  108.5 1.7 %collective-permute-start.26 = (bf16[32,2048]{1,0:T(8,128)(2,1)S(1)}, bf16[32,2048]{1,0:T(8,128)(2,1)S(1)}, u32[]{:S(2)}, u32[]{:S(2)}) collective-permute-start(bf16[32,2048]{1,0:T(8,128)(2,1)S(1)} %get-tuple-element.6), channel_id=1, source_target_pairs={{0,16},{4,20},{8,24},{12,28},{16,0},{20,4},{24,8},{28,12},{1,17},{... | collective-permute-start | bytes 393224 | tf_op jit(solution)/shard_map/ppermute | solution.py:98
  110.2 2.6 %collective-permute-start.27 = (bf16[32,2048]{1,0:T(8,128)(2,1)S(1)}, bf16[32,2048]{1,0:T(8,128)(2,1)S(1)}, u32[]{:S(2)}, u32[]{:S(2)}) collective-permute-start(bf16[32,2048]{1,0:T(8,128)(2,1)S(1)} %get-tuple-element.6), channel_id=1, source_target_pairs={{0,24},{4,28},{8,16},{12,20},{16,8},{20,12},{24,0},{28,4},{1,25},{... | collective-permute-start | bytes 393224 | tf_op jit(solution)/shard_map/ppermute | solution.py:98
  112.9 1.8 %collective-permute-done.25 = bf16[32,2048]{1,0:T(8,128)(2,1)S(1)} collective-permute-done((bf16[32,2048]{1,0:T(8,128)(2,1)S(1)}, bf16[32,2048]{1,0:T(8,128)(2,1)S(1)}, u32[]{:S(2)}, u32[]{:S(2)}) %collective-permute-start.25) | collective-permute-done | bytes 131104 | tf_op jit(solution)/shard_map/ppermute | solution.py:98
  114.7 4.9 %collective-permute-done.26 = bf16[32,2048]{1,0:T(8,128)(2,1)S(1)} collective-permute-done((bf16[32,2048]{1,0:T(8,128)(2,1)S(1)}, bf16[32,2048]{1,0:T(8,128)(2,1)S(1)}, u32[]{:S(2)}, u32[]{:S(2)}) %collective-permute-start.26) | collective-permute-done | bytes 131104 | tf_op jit(solution)/shard_map/ppermute | solution.py:98
  119.7 0.7 multiply_convert_fusion
  120.4 0.1 broadcast_in_dim.141
  120.6 1.0 collective-permute-done.28
  121.6 1.3 convert_bitcast_fusion
  123.0 1.3 convert_bitcast_fusion.1
  124.3 1.3 convert_bitcast_fusion.2
  125.6 5.4 %pad_maximum_fusion = bf16[3,1024,2048]{2,1,0:T(8,128)(2,1)} fusion(bf16[1,1024,2048]{2,1,0:T(8,128)(2,1)S(1)} %convert_bitcast_fusion, bf16[1,1024,2048]{2,1,0:T(8,128)(2,1)S(1)} %convert_bitcast_fusion.1, bf16[1,1024,2048]{2,1,0:T(8,128)(2,1)S(1)} %convert_bitcast_fusion.2), kind=kLoop, calls=%fused_computation.5 | loop fusion | flops 12582912 | bytes 25165824 | tf_op jit(solution)/shard_map/stack | solution.py:105
  (91 shorter events, 1.6 us)
Async XLA Ops:
  0.6 6.8 %copy-start = (bf16[64,8192]{1,0:T(8,128)(2,1)S(1)}, bf16[64,8192]{1,0:T(8,128)(2,1)}, u32[]{:S(2)}) copy-start(bf16[64,8192]{1,0:T(8,128)(2,1)} %param.10) | copy-start | bytes 3145732
  5.6 12.9 %copy-start.3 = (bf16[64,2048]{1,0:T(8,128)(2,1)S(1)}, bf16[64,2048]{1,0:T(8,128)(2,1)}, u32[]{:S(2)}) copy-start(bf16[64,2048]{1,0:T(8,128)(2,1)} %param.11) | copy-start | bytes 786436
  6.1 13.2 %collective-permute-start = (bf16[32,1024]{1,0:T(8,128)(2,1)S(1)}, bf16[32,1024]{1,0:T(8,128)(2,1)S(1)}, u32[]{:S(2)}, u32[]{:S(2)}) collective-permute-start(bf16[32,1024]{1,0:T(8,128)(2,1)S(1)} %bitcast.180), channel_id=1, source_target_pairs={{0,0},{1,8},{2,16},{3,24},{4,4},{5,12},{6,20},{7,28},{8,1},{9,9},{... | collective-permute-start | bytes 196616 | tf_op jit(solution)/shard_map/ppermute | solution.py:58
  6.8 12.5 %collective-permute-start.1 = (bf16[32,1024]{1,0:T(8,128)(2,1)S(1)}, bf16[32,1024]{1,0:T(8,128)(2,1)S(1)}, u32[]{:S(2)}, u32[]{:S(2)}) collective-permute-start(bf16[32,1024]{1,0:T(8,128)(2,1)S(1)} %bitcast.179), channel_id=1, source_target_pairs={{0,4},{1,12},{2,20},{3,28},{4,0},{5,8},{6,16},{7,24},{8,5},{9,13},... | collective-permute-start | bytes 196616 | tf_op jit(solution)/shard_map/ppermute | solution.py:58
  8.5 15.9 %collective-permute-start.10 = (bf16[32,2048]{1,0:T(8,128)(2,1)S(1)}, bf16[32,2048]{1,0:T(8,128)(2,1)S(1)}, u32[]{:S(2)}, u32[]{:S(2)}) collective-permute-start(bf16[32,2048]{1,0:T(8,128)(2,1)S(1)} %get-tuple-element.11), channel_id=1, source_target_pairs={{0,1},{1,0},{2,3},{3,2},{4,5},{5,4},{6,7},{7,6},{8,9},{9,8},{10,11... | collective-permute-start | bytes 393224 | tf_op jit(solution)/shard_map/ppermute | solution.py:15
  14.3 10.6 %collective-permute-start.12 = (bf16[32,2048]{1,0:T(8,128)(2,1)S(1)}, bf16[32,2048]{1,0:T(8,128)(2,1)S(1)}, u32[]{:S(2)}, u32[]{:S(2)}) collective-permute-start(bf16[32,2048]{1,0:T(8,128)(2,1)S(1)} %get-tuple-element.12), channel_id=1, source_target_pairs={{0,3},{1,2},{2,1},{3,0},{4,7},{5,6},{6,5},{7,4},{8,11},{9,10},{10,... | collective-permute-start | bytes 393224 | tf_op jit(solution)/shard_map/ppermute | solution.py:15
  18.1 12.0 %collective-permute-start.11 = (bf16[32,2048]{1,0:T(8,128)(2,1)S(1)}, bf16[32,2048]{1,0:T(8,128)(2,1)S(1)}, u32[]{:S(2)}, u32[]{:S(2)}) collective-permute-start(bf16[32,2048]{1,0:T(8,128)(2,1)S(1)} %get-tuple-element.13), channel_id=1, source_target_pairs={{0,2},{1,3},{2,0},{3,1},{4,6},{5,7},{6,4},{7,5},{8,10},{9,11},{10,... | collective-permute-start | bytes 393224 | tf_op jit(solution)/shard_map/ppermute | solution.py:15
  19.4 41.8 %collective-permute-start.4 = (bf16[64,1024]{1,0:T(8,128)(2,1)S(1)}, bf16[64,1024]{1,0:T(8,128)(2,1)S(1)}, u32[]{:S(2)}, u32[]{:S(2)}) collective-permute-start(bf16[64,1024]{1,0:T(8,128)(2,1)S(1)} %bitcast.167), channel_id=1, source_target_pairs={{0,3},{1,2},{2,1},{3,0},{4,7},{5,6},{6,5},{7,4},{8,11},{9,10},{10,... | collective-permute-start | bytes 393224 | tf_op jit(solution)/shard_map/ppermute | solution.py:15
  23.7 36.8 %collective-permute-start.3 = (bf16[64,1024]{1,0:T(8,128)(2,1)S(1)}, bf16[64,1024]{1,0:T(8,128)(2,1)S(1)}, u32[]{:S(2)}, u32[]{:S(2)}) collective-permute-start(bf16[64,1024]{1,0:T(8,128)(2,1)S(1)} %bitcast.168), channel_id=1, source_target_pairs={{0,2},{1,3},{2,0},{3,1},{4,6},{5,7},{6,4},{7,5},{8,10},{9,11},{10,... | collective-permute-start | bytes 393224 | tf_op jit(solution)/shard_map/ppermute | solution.py:15
  24.3 9.7 %collective-permute-start.2 = (bf16[64,1024]{1,0:T(8,128)(2,1)S(1)}, bf16[64,1024]{1,0:T(8,128)(2,1)S(1)}, u32[]{:S(2)}, u32[]{:S(2)}) collective-permute-start(bf16[64,1024]{1,0:T(8,128)(2,1)S(1)} %bitcast.169), channel_id=1, source_target_pairs={{0,1},{1,0},{2,3},{3,2},{4,5},{5,4},{6,7},{7,6},{8,9},{9,8},{10,11... | collective-permute-start | bytes 393224 | tf_op jit(solution)/shard_map/ppermute | solution.py:15
  30.8 0.9 collective-permute-start.13
  31.7 23.7 %collective-permute-start.6 = (bf16[32,1024]{1,0:T(8,128)(2,1)S(1)}, bf16[32,1024]{1,0:T(8,128)(2,1)S(1)}, u32[]{:S(2)}, u32[]{:S(2)}) collective-permute-start(bf16[32,1024]{1,0:T(8,128)(2,1)S(1)} %bitcast.181), channel_id=1, source_target_pairs={{0,4},{1,12},{2,20},{3,28},{4,0},{5,8},{6,16},{7,24},{8,5},{9,13},... | collective-permute-start | bytes 196616 | tf_op jit(solution)/shard_map/ppermute | solution.py:58
  31.8 1.4 %collective-permute-start.14 = (bf16[32,1024]{1,0:T(8,128)(2,1)S(1)}, bf16[32,1024]{1,0:T(8,128)(2,1)S(1)}, u32[]{:S(2)}, u32[]{:S(2)}) collective-permute-start(bf16[32,1024]{1,0:T(8,128)(2,1)S(1)} %bitcast.183), channel_id=1, source_target_pairs={{0,4},{1,12},{2,20},{3,28},{4,0},{5,8},{6,16},{7,24},{8,5},{9,13},... | collective-permute-start | bytes 196616 | tf_op jit(solution)/shard_map/ppermute | solution.py:58
  33.2 21.6 %collective-permute-start.5 = (bf16[32,1024]{1,0:T(8,128)(2,1)S(1)}, bf16[32,1024]{1,0:T(8,128)(2,1)S(1)}, u32[]{:S(2)}, u32[]{:S(2)}) collective-permute-start(bf16[32,1024]{1,0:T(8,128)(2,1)S(1)} %bitcast.182), channel_id=1, source_target_pairs={{0,0},{1,8},{2,16},{3,24},{4,4},{5,12},{6,20},{7,28},{8,1},{9,9},{... | collective-permute-start | bytes 196616 | tf_op jit(solution)/shard_map/ppermute | solution.py:58
  34.0 32.3 %collective-permute-start.17 = (bf16[64,1024]{1,0:T(8,128)(2,1)S(1)}, bf16[64,1024]{1,0:T(8,128)(2,1)S(1)}, u32[]{:S(2)}, u32[]{:S(2)}) collective-permute-start(bf16[64,1024]{1,0:T(8,128)(2,1)S(1)} %bitcast.171), channel_id=1, source_target_pairs={{0,3},{1,2},{2,1},{3,0},{4,7},{5,6},{6,5},{7,4},{8,11},{9,10},{10,... | collective-permute-start | bytes 393224 | tf_op jit(solution)/shard_map/ppermute | solution.py:15
  54.8 11.5 %collective-permute-start.16 = (bf16[64,1024]{1,0:T(8,128)(2,1)S(1)}, bf16[64,1024]{1,0:T(8,128)(2,1)S(1)}, u32[]{:S(2)}, u32[]{:S(2)}) collective-permute-start(bf16[64,1024]{1,0:T(8,128)(2,1)S(1)} %bitcast.172), channel_id=1, source_target_pairs={{0,2},{1,3},{2,0},{3,1},{4,6},{5,7},{6,4},{7,5},{8,10},{9,11},{10,... | collective-permute-start | bytes 393224 | tf_op jit(solution)/shard_map/ppermute | solution.py:15
  55.4 8.6 %collective-permute-start.15 = (bf16[64,1024]{1,0:T(8,128)(2,1)S(1)}, bf16[64,1024]{1,0:T(8,128)(2,1)S(1)}, u32[]{:S(2)}, u32[]{:S(2)}) collective-permute-start(bf16[64,1024]{1,0:T(8,128)(2,1)S(1)} %bitcast.173), channel_id=1, source_target_pairs={{0,1},{1,0},{2,3},{3,2},{4,5},{5,4},{6,7},{7,6},{8,9},{9,8},{10,11... | collective-permute-start | bytes 393224 | tf_op jit(solution)/shard_map/ppermute | solution.py:15
  60.5 9.6 %collective-permute-start.9 = (bf16[64,1024]{1,0:T(8,128)(2,1)S(1)}, bf16[64,1024]{1,0:T(8,128)(2,1)S(1)}, u32[]{:S(2)}, u32[]{:S(2)}) collective-permute-start(bf16[64,1024]{1,0:T(8,128)(2,1)S(1)} %bitcast.175), channel_id=1, source_target_pairs={{0,3},{1,2},{2,1},{3,0},{4,7},{5,6},{6,5},{7,4},{8,11},{9,10},{10,... | collective-permute-start | bytes 393224 | tf_op jit(solution)/shard_map/ppermute | solution.py:15
  61.1 8.9 %collective-permute-start.8 = (bf16[64,1024]{1,0:T(8,128)(2,1)S(1)}, bf16[64,1024]{1,0:T(8,128)(2,1)S(1)}, u32[]{:S(2)}, u32[]{:S(2)}) collective-permute-start(bf16[64,1024]{1,0:T(8,128)(2,1)S(1)} %bitcast.176), channel_id=1, source_target_pairs={{0,2},{1,3},{2,0},{3,1},{4,6},{5,7},{6,4},{7,5},{8,10},{9,11},{10,... | collective-permute-start | bytes 393224 | tf_op jit(solution)/shard_map/ppermute | solution.py:15
  62.1 11.6 %copy-start.1 = (bf16[4,64,1024]{2,1,0:T(8,128)(2,1)}, bf16[4,64,1024]{2,1,0:T(8,128)(2,1)S(1)}, u32[]{:S(2)}) copy-start(bf16[4,64,1024]{2,1,0:T(8,128)(2,1)S(1)} %bitcast_dynamic-update-slice_fusion.14) | copy-start | bytes 1572868
  63.9 6.0 %collective-permute-start.7 = (bf16[64,1024]{1,0:T(8,128)(2,1)S(1)}, bf16[64,1024]{1,0:T(8,128)(2,1)S(1)}, u32[]{:S(2)}, u32[]{:S(2)}) collective-permute-start(bf16[64,1024]{1,0:T(8,128)(2,1)S(1)} %bitcast.178), channel_id=1, source_target_pairs={{0,1},{1,0},{2,3},{3,2},{4,5},{5,4},{6,7},{7,6},{8,9},{9,8},{10,11... | collective-permute-start | bytes 393224 | tf_op jit(solution)/shard_map/ppermute | solution.py:15
  66.3 3.8 %copy-start.4 = (bf16[4,64,1024]{2,1,0:T(8,128)(2,1)}, bf16[4,64,1024]{2,1,0:T(8,128)(2,1)S(1)}, u32[]{:S(2)}) copy-start(bf16[4,64,1024]{2,1,0:T(8,128)(2,1)S(1)} %bitcast_dynamic-update-slice_fusion.6) | copy-start | bytes 1572868
  70.1 3.7 %copy-start.6 = (bf16[4,64,1024]{2,1,0:T(8,128)(2,1)}, bf16[4,64,1024]{2,1,0:T(8,128)(2,1)S(1)}, u32[]{:S(2)}) copy-start(bf16[4,64,1024]{2,1,0:T(8,128)(2,1)S(1)} %bitcast_dynamic-update-slice_fusion.10) | copy-start | bytes 1572868
  77.3 21.7 %copy-start.9 = (bf16[32,2048]{1,0:T(8,128)(2,1)S(1)}, bf16[32,2048]{1,0:T(8,128)(2,1)}, u32[]{:S(2)}) copy-start(bf16[32,2048]{1,0:T(8,128)(2,1)} %param.17) | copy-start | bytes 393220
  77.3 21.6 %copy-start.10 = (f32[2048]{0:T(1024)S(1)}, f32[2048]{0:T(1024)}, u32[]{:S(2)}) copy-start(f32[2048]{0:T(1024)} %param.16) | copy-start | bytes 24580
  78.4 3.0 %collective-permute-start.18 = (f32[4,32,2048]{2,1,0:T(8,128)}, f32[4,32,2048]{2,1,0:T(8,128)}, u32[]{:S(2)}, u32[]{:S(2)}) collective-permute-start(f32[4,32,2048]{2,1,0:T(8,128)} %dynamic-slice_bitcast_fusion), channel_id=1, source_target_pairs={{0,4},{4,0},{8,12},{12,8},{16,20},{20,16},{24,28},{28,24},{1,5},{5... | collective-permute-start | bytes 3145736 | tf_op jit(solution)/shard_map/ppermute | solution.py:76
  82.8 1.0 copy-start.8
  83.7 37.9 %copy-start.5 = (bf16[4,64,1024]{2,1,0:T(8,128)(2,1)S(1)}, bf16[4,64,1024]{2,1,0:T(8,128)(2,1)}, u32[]{:S(2)}) copy-start(bf16[4,64,1024]{2,1,0:T(8,128)(2,1)} %copy-done.4) | copy-start | bytes 1572868
  83.8 5.6 %collective-permute-start.19 = (bf16[32,2048]{1,0:T(8,128)(2,1)S(1)}, bf16[32,2048]{1,0:T(8,128)(2,1)S(1)}, u32[]{:S(2)}, u32[]{:S(2)}) collective-permute-start(bf16[32,2048]{1,0:T(8,128)(2,1)S(1)} %get-tuple-element.8), channel_id=1, source_target_pairs={{0,8},{4,12},{8,0},{12,4},{16,24},{20,28},{24,16},{28,20},{1,9},{5... | collective-permute-start | bytes 393224 | tf_op jit(solution)/shard_map/ppermute | solution.py:82
  83.9 9.9 %collective-permute-start.21 = (bf16[32,2048]{1,0:T(8,128)(2,1)S(1)}, bf16[32,2048]{1,0:T(8,128)(2,1)S(1)}, u32[]{:S(2)}, u32[]{:S(2)}) collective-permute-start(bf16[32,2048]{1,0:T(8,128)(2,1)S(1)} %get-tuple-element.9), channel_id=1, source_target_pairs={{0,24},{4,28},{8,16},{12,20},{16,8},{20,12},{24,0},{28,4},{1,25},{... | collective-permute-start | bytes 393224 | tf_op jit(solution)/shard_map/ppermute | solution.py:82
  86.6 12.4 %collective-permute-start.20 = (bf16[32,2048]{1,0:T(8,128)(2,1)S(1)}, bf16[32,2048]{1,0:T(8,128)(2,1)S(1)}, u32[]{:S(2)}, u32[]{:S(2)}) collective-permute-start(bf16[32,2048]{1,0:T(8,128)(2,1)S(1)} %get-tuple-element.10), channel_id=1, source_target_pairs={{0,16},{4,20},{8,24},{12,28},{16,0},{20,4},{24,8},{28,12},{1,17},{... | collective-permute-start | bytes 393224 | tf_op jit(solution)/shard_map/ppermute | solution.py:82
  100.2 3.6 %collective-permute-start.23 = (f32[2,32]{1,0:T(2,128)S(1)}, f32[2,32]{1,0:T(2,128)S(1)}, u32[]{:S(2)}, u32[]{:S(2)}) collective-permute-start(f32[2,32]{1,0:T(2,128)S(1)} %get-tuple-element.21), channel_id=1, source_target_pairs={{0,2},{1,3},{2,0},{3,1},{4,6},{5,7},{6,4},{7,5},{8,10},{9,11},{10,... | collective-permute-start | bytes 776 | tf_op jit(solution)/shard_map/ppermute | solution.py:15
  101.9 3.6 %collective-permute-start.22 = (f32[2,32]{1,0:T(2,128)S(1)}, f32[2,32]{1,0:T(2,128)S(1)}, u32[]{:S(2)}, u32[]{:S(2)}) collective-permute-start(f32[2,32]{1,0:T(2,128)S(1)} %get-tuple-element.21), channel_id=1, source_target_pairs={{0,1},{1,0},{2,3},{3,2},{4,5},{5,4},{6,7},{7,6},{8,9},{9,8},{10,11... | collective-permute-start | bytes 776 | tf_op jit(solution)/shard_map/ppermute | solution.py:15
  103.1 4.5 %collective-permute-start.24 = (f32[2,32]{1,0:T(2,128)S(1)}, f32[2,32]{1,0:T(2,128)S(1)}, u32[]{:S(2)}, u32[]{:S(2)}) collective-permute-start(f32[2,32]{1,0:T(2,128)S(1)} %get-tuple-element.21), channel_id=1, source_target_pairs={{0,3},{1,2},{2,1},{3,0},{4,7},{5,6},{6,5},{7,4},{8,11},{9,10},{10,... | collective-permute-start | bytes 776 | tf_op jit(solution)/shard_map/ppermute | solution.py:15
  108.4 6.2 %collective-permute-start.25 = (bf16[32,2048]{1,0:T(8,128)(2,1)S(1)}, bf16[32,2048]{1,0:T(8,128)(2,1)S(1)}, u32[]{:S(2)}, u32[]{:S(2)}) collective-permute-start(bf16[32,2048]{1,0:T(8,128)(2,1)S(1)} %get-tuple-element.6), channel_id=1, source_target_pairs={{0,8},{4,12},{8,0},{12,4},{16,24},{20,28},{24,16},{28,20},{1,9},{5... | collective-permute-start | bytes 393224 | tf_op jit(solution)/shard_map/ppermute | solution.py:98
  108.5 11.0 %collective-permute-start.26 = (bf16[32,2048]{1,0:T(8,128)(2,1)S(1)}, bf16[32,2048]{1,0:T(8,128)(2,1)S(1)}, u32[]{:S(2)}, u32[]{:S(2)}) collective-permute-start(bf16[32,2048]{1,0:T(8,128)(2,1)S(1)} %get-tuple-element.6), channel_id=1, source_target_pairs={{0,16},{4,20},{8,24},{12,28},{16,0},{20,4},{24,8},{28,12},{1,17},{... | collective-permute-start | bytes 393224 | tf_op jit(solution)/shard_map/ppermute | solution.py:98
  110.2 9.3 %collective-permute-start.27 = (bf16[32,2048]{1,0:T(8,128)(2,1)S(1)}, bf16[32,2048]{1,0:T(8,128)(2,1)S(1)}, u32[]{:S(2)}, u32[]{:S(2)}) collective-permute-start(bf16[32,2048]{1,0:T(8,128)(2,1)S(1)} %get-tuple-element.6), channel_id=1, source_target_pairs={{0,24},{4,28},{8,16},{12,20},{16,8},{20,12},{24,0},{28,4},{1,25},{... | collective-permute-start | bytes 393224 | tf_op jit(solution)/shard_map/ppermute | solution.py:98
  119.6 2.0 %collective-permute-start.28 = (bf16[4,32,2048]{2,1,0:T(8,128)(2,1)S(1)}, bf16[4,32,2048]{2,1,0:T(8,128)(2,1)S(1)}, u32[]{:S(2)}, u32[]{:S(2)}) collective-permute-start(bf16[4,32,2048]{2,1,0:T(8,128)(2,1)S(1)} %bitcast_dynamic-update-slice_fusion.2), channel_id=1, source_target_pairs={{0,4},{4,0},{8,12},{12,8},{16,20},{20,16},{24,28},{28,24},{1,5},{5... | collective-permute-start | bytes 1572872 | tf_op jit(solution)/shard_map/ppermute | solution.py:100
  120.5 2.4 %copy-start.7 = (bf16[4,64,1024]{2,1,0:T(8,128)(2,1)S(1)}, bf16[4,64,1024]{2,1,0:T(8,128)(2,1)}, u32[]{:S(2)}) copy-start(bf16[4,64,1024]{2,1,0:T(8,128)(2,1)} %copy-done.6) | copy-start | bytes 1572868
  122.9 1.3 copy-start.2
